TPU v7x, 32 devices: a whole 2x2x4 slice. The times are simulated.
32 devices in a mesh: group: 2 (over x), sector: 16 (over z, y, core).
Axes of the slice: x: 2, y: 2, z: 4, core: 2. Of those that a mesh axis runs over, the one named last changes fastest.
Arguments:
- wave: bfloat16 [32, 16, 256, 256], P(('group', 'sector')), parts along dimension 0, may hold values from -6 to 6
- left_ops: bfloat16 [384, 256, 256], P(('group', 'sector')), parts along dimension 0, may hold values from -0.375 to 0.375
- right_ops: bfloat16 [384, 256, 256], P(('group', 'sector')), parts along dimension 0, may hold values from -0.375 to 0.375
- deltas: int32 [384], P(('group', 'sector')), parts along dimension 0, may hold values from -1 to 1, as said below
- counts: int32 [32], P(('group', 'sector')), parts along dimension 0, may hold values from 2 to 12, as said below
Outputs:
- sigma: bfloat16 [32, 16, 256, 256], P(('group', 'sector')), parts along dimension 0
There are 2 independent parts, one for each index of `group`. A program takes and returns all parts, laid end to end along the dimension named above; each array names one. Nothing has to cross between parts.
Inputs may be any that keep to these rules, and one draw needn't show every extreme that they name: `counts`: some sector has exactly 12 live slots in every draw; slots at or beyond a sector's count are unused. Every sector has 2 or more live slots. In each aligned pair of sectors 2i and 2i + 1 at most one has more than 6 live slots, and every other sector has 2 or 3 live slots. `deltas`: slot 0 of every sector reads the sector below it (offset -1) and slot 1 the sector above it (offset +1).
All inputs are finite; a program needn't handle non-finite values.
Results may differ from a plain program's by a relative error of at most 0.0049.
Values may be sent and summed in bfloat16 or wider, within the bound.
No kernel may reach another device: no remote copies, remote signals or barrier semaphores. Data moves between devices by JAX's collectives and lax.ppermute only.
A program may use at most 64 MiB of HBM per device.

v0:
```python
import functools

import jax
import jax.numpy as jnp
from jax import lax
from jax.experimental import pallas as pl
from jax.experimental.pallas import tpu as pltpu
from jax.sharding import PartitionSpec as P


def source_of(delta, parity, mine_first, phase):
    pos = jnp.clip(delta, -1, 1) + 1 + (parity if mine_first else 1 - parity)
    phys = jnp.where(parity == 0, pos + 1 - 2 * (pos % 2), (pos + 2) % 4)
    if phase == 0:
        return jnp.where(phys == 0, 0, jnp.where(phys == 3, 1, 2))
    return jnp.where(phys == phase, 0, 2)


def pairs_kernel(phase, n_src, *refs):
    d_own, c_own, d_par, c_par = refs[:4]
    srcs = refs[4:4 + n_src]
    l_own, r_own, l_par, r_par = refs[4 + n_src:8 + n_src]
    rest = refs[8 + n_src:]
    if phase > 0:
        s_own, s_par = rest[:2]
        rest = rest[2:]
    else:
        s_own = s_par = None
    o_own, o_par, acc_ref, mixed_ref = rest
    rows, width = srcs[0].shape[0], srcs[0].shape[1]
    size = rows * width
    parity = lax.axis_index("sector") % 2
    jobs = (
        (False, d_par, c_par, l_par, r_par, s_par, o_par),
        (True, d_own, c_own, l_own, r_own, s_own, o_own),
    )
    for mine_first, deltas_ref, count_ref, left_ref, right_ref, start_ref, out_ref in jobs:
        if start_ref is None:
            acc_ref[...] = jnp.zeros_like(acc_ref)
        else:
            acc_ref[...] = start_ref[...]

        def step(k, carry, deltas_ref=deltas_ref, left_ref=left_ref, right_ref=right_ref, mine_first=mine_first):
            which = source_of(deltas_ref[k], parity, mine_first, phase)

            @pl.when(which < n_src)
            def _():
                left = left_ref[k]

                def run(src_ref):
                    for r in range(rows):
                        mixed_ref[pl.ds(r * width, width), :] = jnp.dot(
                            left, src_ref[r], preferred_element_type=jnp.float32
                        ).astype(jnp.bfloat16)

                for m, ref in enumerate(srcs):
                    pl.when(which == m)(functools.partial(run, ref))
                acc_ref[...] += lax.dot_general(
                    mixed_ref[...], right_ref[k], (((1,), (1,)), ((), ())), preferred_element_type=jnp.float32
                )

            return carry

        lax.fori_loop(0, jnp.minimum(count_ref[0], left_ref.shape[0]), step, 0)
        if phase == 2 and mine_first:
            offset = pl.multiple_of(parity * size, size)
            out_ref[pl.ds(offset, size), :] = acc_ref[...].astype(out_ref.dtype)
        else:
            out_ref[...] = acc_ref[...].astype(out_ref.dtype)


def apply_pairs(phase, sources, own_job, partner_job, starts=()):
    rows, width = sources[0].shape[0], sources[0].shape[1]
    size = rows * width
    left_ops, right_ops, deltas, counts = own_job
    left_p, right_p, deltas_p, counts_p = partner_job
    slots = left_ops.shape[0]
    vmem = pl.BlockSpec(memory_space=pltpu.VMEM)
    smem = pl.BlockSpec(memory_space=pltpu.SMEM)
    flops = 4 * slots * size * width * width // 2
    moved = 2 * (len(sources) * size * width + 4 * slots * width * width) + 16 * size * width
    if phase == 2:
        outs = (
            jax.ShapeDtypeStruct((2 * size, width), jnp.bfloat16),
            jax.ShapeDtypeStruct((size, width), jnp.bfloat16),
        )
    else:
        outs = (jax.ShapeDtypeStruct((size, width), jnp.float32),) * 2
    return pl.pallas_call(
        functools.partial(pairs_kernel, phase, len(sources)),
        out_shape=outs,
        in_specs=[smem] * 4 + [vmem] * (len(sources) + 4 + len(starts)),
        out_specs=(vmem, vmem),
        scratch_shapes=[
            pltpu.VMEM((size, width), jnp.float32),
            pltpu.VMEM((size, width), jnp.bfloat16),
        ],
        cost_estimate=pl.CostEstimate(flops=flops, bytes_accessed=moved, transcendentals=0),
    )(deltas, counts, deltas_p, counts_p, *sources, left_ops, right_ops, left_p, right_p, *starts)


def on_device(wave, left_ops, right_ops, deltas, counts):
    n = lax.axis_size("sector")
    me = lax.axis_index("sector")
    parity = me % 2
    own = wave[0]
    half = own.shape[0] // 2
    mine = lax.dynamic_slice_in_dim(own, parity * half, half, 0)
    other = lax.dynamic_slice_in_dim(own, (1 - parity) * half, half, 0)

    odd, even = range(1, n, 2), range(0, n, 2)
    near = [(j, j + 1) for j in odd if j + 1 < n] + [(j, j - 1) for j in even if j >= 2]
    far = [(j, j + 2) for j in odd if j + 2 < n] + [(j, j - 2) for j in even if j >= 2]
    partner = [(j, j ^ 1) for j in range(n)]

    from_near = lax.ppermute(other, "sector", near)
    from_far = lax.ppermute(mine, "sector", far)
    from_partner = lax.ppermute(other, "sector", partner)

    left_p = lax.ppermute(left_ops, "sector", partner)
    right_p = lax.ppermute(right_ops, "sector", partner)
    deltas_p = lax.ppermute(deltas, "sector", partner)
    counts_p = lax.ppermute(counts, "sector", partner)
    own_job = (left_ops, right_ops, deltas, counts)
    partner_job = (left_p, right_p, deltas_p, counts_p)

    own_sum, partner_sum = apply_pairs(0, (mine, from_partner), own_job, partner_job)
    own_sum, partner_sum, from_near = lax.optimization_barrier((own_sum, partner_sum, from_near))
    own_sum, partner_sum = apply_pairs(1, (from_near,), own_job, partner_job, (own_sum, partner_sum))
    own_sum, partner_sum, from_far = lax.optimization_barrier((own_sum, partner_sum, from_far))
    out, partner_half = apply_pairs(2, (from_far,), own_job, partner_job, (own_sum, partner_sum))

    returned = lax.ppermute(partner_half.reshape((half,) + own.shape[1:]), "sector", partner)
    out = lax.dynamic_update_slice_in_dim(out.reshape(own.shape), returned, (1 - parity) * half, 0)
    return out[None]


def solution(mesh):
    return jax.shard_map(
        on_device,
        mesh=mesh,
        in_specs=(
            P(("group", "sector"), None, None, None),
            P(("group", "sector"), None, None),
            P(("group", "sector"), None, None),
            P(("group", "sector")),
            P(("group", "sector")),
        ),
        out_specs=P(("group", "sector"), None, None, None),
        check_vma=False,
    )
```

profile of v0, /device:TPU:7, one launch (start us, length us, event | category | flops | bytes accessed | tf_op | source)
XLA Modules:
  0.0 69.0 jit_solution(7751712536413632636)
XLA Ops:
  0.0 0.7 collective-permute-start.3
  0.7 0.0 collective-permute-start.4
  0.7 1.7 %dynamic-slice_bitcast_fusion = (bf16[8,256,256]{2,1,0:T(8,128)(2,1)S(1)}, bf16[8,256,256]{2,1,0:T(8,128)(2,1)S(1)}) fusion(bf16[1,16,256,256]{3,2,1,0:T(8,128)(2,1)} %param.5, s32[]{:T(128)S(6)} %select_n.16, s32[]{:T(128)S(6)} %select_n.15), kind=kLoop, calls=%fused_computation.1 | loop fusion | bytes 4194312 | tf_op jit(solution)/shard_map/dynamic_slice | solution.py:109
  2.4 0.0 copy-start
  2.4 0.6 collective-permute-start.2
  3.0 3.0 %collective-permute-start.5 = (bf16[8,256,256]{2,1,0:T(8,128)(2,1)S(1)}, bf16[8,256,256]{2,1,0:T(8,128)(2,1)S(1)}, u32[]{:S(2)}, u32[]{:S(2)}) collective-permute-start(bf16[8,256,256]{2,1,0:T(8,128)(2,1)S(1)} %get-tuple-element.29), channel_id=1, source_target_pairs={{1,2},{3,4},{5,6},{7,8},{9,10},{11,12},{13,14},{2,1},{4,3},{6,5},{... | collective-permute-start | bytes 3145736 | tf_op jit(solution)/shard_map/ppermute | solution.py:116
  6.0 0.1 collective-permute-start.1
  6.1 1.6 %collective-permute-done.1.refs_3_ = s32[1]{0:T(128)} collective-permute-done((s32[1]{0:T(128)}, s32[1]{0:T(128)}, u32[]{:S(2)}, u32[]{:S(2)}) %collective-permute-start.1) | collective-permute-done | bytes 36 | tf_op jit(solution)/shard_map/ppermute | solution.py:123
  7.7 0.3 collective-permute-start
  8.1 0.8 %collective-permute-done.refs_2_ = s32[12]{0:T(128)S(1)} collective-permute-done((s32[12]{0:T(128)S(1)}, s32[12]{0:T(128)S(1)}, u32[]{:S(2)}, u32[]{:S(2)}) %collective-permute-start) | collective-permute-done | bytes 80 | tf_op jit(solution)/shard_map/ppermute | solution.py:122
  8.9 3.1 %collective-permute-start.6 = (bf16[8,256,256]{2,1,0:T(8,128)(2,1)S(1)}, bf16[8,256,256]{2,1,0:T(8,128)(2,1)}, u32[]{:S(2)}, u32[]{:S(2)}) collective-permute-start(bf16[8,256,256]{2,1,0:T(8,128)(2,1)S(1)} %get-tuple-element.30.refs_4_), channel_id=1, source_target_pairs={{1,3},{3,5},{5,7},{7,9},{9,11},{11,13},{13,15},{2,0},{4,2},{6,4},{... | collective-permute-start | bytes 3145736 | tf_op jit(solution)/shard_map/ppermute | solution.py:117
  12.7 0.0 collective-permute-done.2.refs_5_
  12.7 1.0 %copy-done.2 = bf16[8,256,256]{2,1,0:T(8,128)(2,1)} copy-done((bf16[8,256,256]{2,1,0:T(8,128)(2,1)}, bf16[8,256,256]{2,1,0:T(8,128)(2,1)S(1)}, u32[]{:S(2)}) %copy-start.2) | copy-done | bytes 1048600
  13.7 0.0 collective-permute-done.3.refs_8_.refs_7_
  13.7 0.0 collective-permute-done.4.refs_9_.refs_8_
  13.7 14.2 %shard_map.55 = (f32[2048,256]{1,0:T(8,128)}, f32[2048,256]{1,0:T(8,128)}) custom-call(s32[12]{0:T(128)} %refs_0_.5, s32[1]{0:T(128)S(6)} %copy.7.refs_1_, s32[12]{0:T(128)} %copy-done.4, s32[1]{0:T(128)} %collective-permute-done.1.refs_3_, bf16[8,256,256]{2,1,0:T(8,128)(2,1)} %copy-done, bf16[8,256,256]{2,1,0:T(8,128)(2,1)} %copy-done.2, ...), custom_call_target="tpu_custom_call" | custom-call | flops 3221225472 | bytes 16777216 | tf_op jit(solution)/shard_map/pallas_call | solution.py:89
  27.9 0.0 collective-permute-done.5.refs_4_
  27.9 1.0 %copy-done.1 = bf16[8,256,256]{2,1,0:T(8,128)(2,1)} copy-done((bf16[8,256,256]{2,1,0:T(8,128)(2,1)}, bf16[8,256,256]{2,1,0:T(8,128)(2,1)S(1)}, u32[]{:S(2)}) %copy-start.1) | copy-done | bytes 1048600
  28.8 8.6 %shard_map.56 = (f32[2048,256]{1,0:T(8,128)}, f32[2048,256]{1,0:T(8,128)}) custom-call(s32[12]{0:T(128)} %refs_0_.5, s32[1]{0:T(128)S(6)} %copy.7.refs_1_, s32[12]{0:T(128)} %copy-done.4, s32[1]{0:T(128)} %collective-permute-done.1.refs_3_, bf16[8,256,256]{2,1,0:T(8,128)(2,1)} %copy-done.1, bf16[12,256,256]{2,1,0:T(8,128)(2,1)} %refs_5_.3, ...), custom_call_target="tpu_custom_call" | custom-call | flops 3221225472 | bytes 15728640 | tf_op jit(solution)/shard_map/pallas_call | solution.py:89
  37.5 14.7 %collective-permute-done.6.refs_4_ = bf16[8,256,256]{2,1,0:T(8,128)(2,1)} collective-permute-done((bf16[8,256,256]{2,1,0:T(8,128)(2,1)S(1)}, bf16[8,256,256]{2,1,0:T(8,128)(2,1)}, u32[]{:S(2)}, u32[]{:S(2)}) %collective-permute-start.6) | collective-permute-done | bytes 1048608 | tf_op jit(solution)/shard_map/ppermute | solution.py:117
  52.2 12.8 %shard_map.57 = (bf16[4096,256]{1,0:T(8,128)(2,1)}, bf16[2048,256]{1,0:T(8,128)(2,1)}) custom-call(s32[12]{0:T(128)} %refs_0_.5, s32[1]{0:T(128)S(6)} %copy.7.refs_1_, s32[12]{0:T(128)} %copy-done.4, s32[1]{0:T(128)} %collective-permute-done.1.refs_3_, bf16[8,256,256]{2,1,0:T(8,128)(2,1)} %collective-permute-done.6.refs_4_, bf16[12,256,256]{2,1,0:T(8,128)(2,1)} %refs_5_.3, ...), custom_call_target="tpu_custom_call" | custom-call | flops 3221225472 | bytes 15728640 | tf_op jit(solution)/shard_map/pallas_call | solution.py:89
  65.0 0.0 collective-permute-start.7
  65.0 2.9 %collective-permute-done.7 = bf16[8,256,256]{2,1,0:T(8,128)(2,1)S(1)} collective-permute-done((bf16[8,256,256]{2,1,0:T(8,128)(2,1)}, bf16[8,256,256]{2,1,0:T(8,128)(2,1)S(1)}, u32[]{:S(2)}, u32[]{:S(2)}) %collective-permute-start.7) | collective-permute-done | bytes 1048608 | tf_op jit(solution)/shard_map/ppermute | solution.py:133
  67.9 1.0 %bitcast_dynamic-update-slice_fusion = bf16[1,16,256,256]{3,2,1,0:T(8,128)(2,1)} fusion(bf16[1,16,256,256]{3,2,1,0:T(8,128)(2,1)} %bitcast.8, s32[]{:T(128)S(6)} %select_n.16, bf16[8,256,256]{2,1,0:T(8,128)(2,1)S(1)} %collective-permute-done.7), kind=kLoop, calls=%fused_computation | loop fusion | bytes 2097156 | tf_op jit(solution)/shard_map/dynamic_update_slice | solution.py:134
  (7 shorter events, 0.0 us)
Async XLA Ops:
  0.0 13.7 %collective-permute-start.3 = (bf16[12,256,256]{2,1,0:T(8,128)(2,1)}, bf16[12,256,256]{2,1,0:T(8,128)(2,1)}, u32[]{:S(2)}, u32[]{:S(2)}) collective-permute-start(bf16[12,256,256]{2,1,0:T(8,128)(2,1)} %refs_5_.3), channel_id=1, source_target_pairs={{0,1},{1,0},{2,3},{3,2},{4,5},{5,4},{6,7},{7,6},{8,9},{9,8},{10,11... | collective-permute-start | bytes 4718600 | tf_op jit(solution)/shard_map/ppermute | solution.py:120
  0.7 13.0 %collective-permute-start.4 = (bf16[12,256,256]{2,1,0:T(8,128)(2,1)}, bf16[12,256,256]{2,1,0:T(8,128)(2,1)}, u32[]{:S(2)}, u32[]{:S(2)}) collective-permute-start(bf16[12,256,256]{2,1,0:T(8,128)(2,1)} %refs_6_.5), channel_id=1, source_target_pairs={{0,1},{1,0},{2,3},{3,2},{4,5},{5,4},{6,7},{7,6},{8,9},{9,8},{10,11... | collective-permute-start | bytes 4718600 | tf_op jit(solution)/shard_map/ppermute | solution.py:121
  0.7 7.1 %copy-start.3 = (s32[12]{0:T(128)S(1)}, s32[12]{0:T(128)}, u32[]{:S(2)}) copy-start(s32[12]{0:T(128)} %refs_0_.5) | copy-start | bytes 148
  2.4 11.3 %copy-start = (bf16[8,256,256]{2,1,0:T(8,128)(2,1)}, bf16[8,256,256]{2,1,0:T(8,128)(2,1)S(1)}, u32[]{:S(2)}) copy-start(bf16[8,256,256]{2,1,0:T(8,128)(2,1)S(1)} %get-tuple-element.30.refs_4_) | copy-start | bytes 3145732
  2.4 10.3 %collective-permute-start.2 = (bf16[8,256,256]{2,1,0:T(8,128)(2,1)S(1)}, bf16[8,256,256]{2,1,0:T(8,128)(2,1)S(1)}, u32[]{:S(2)}, u32[]{:S(2)}) collective-permute-start(bf16[8,256,256]{2,1,0:T(8,128)(2,1)S(1)} %get-tuple-element.29), channel_id=1, source_target_pairs={{0,1},{1,0},{2,3},{3,2},{4,5},{5,4},{6,7},{7,6},{8,9},{9,8},{10,11... | collective-permute-start | bytes 3145736 | tf_op jit(solution)/shard_map/ppermute | solution.py:118
  3.0 24.9 %collective-permute-start.5 = (bf16[8,256,256]{2,1,0:T(8,128)(2,1)S(1)}, bf16[8,256,256]{2,1,0:T(8,128)(2,1)S(1)}, u32[]{:S(2)}, u32[]{:S(2)}) collective-permute-start(bf16[8,256,256]{2,1,0:T(8,128)(2,1)S(1)} %get-tuple-element.29), channel_id=1, source_target_pairs={{1,2},{3,4},{5,6},{7,8},{9,10},{11,12},{13,14},{2,1},{4,3},{6,5},{... | collective-permute-start | bytes 3145736 | tf_op jit(solution)/shard_map/ppermute | solution.py:116
  6.0 1.7 %collective-permute-start.1 = (s32[1]{0:T(128)}, s32[1]{0:T(128)}, u32[]{:S(2)}, u32[]{:S(2)}) collective-permute-start(s32[1]{0:T(128)} %param.9), channel_id=1, source_target_pairs={{0,1},{1,0},{2,3},{3,2},{4,5},{5,4},{6,7},{7,6},{8,9},{9,8},{10,11... | collective-permute-start | bytes 20 | tf_op jit(solution)/shard_map/ppermute | solution.py:123
  7.7 1.2 %collective-permute-start = (s32[12]{0:T(128)S(1)}, s32[12]{0:T(128)S(1)}, u32[]{:S(2)}, u32[]{:S(2)}) collective-permute-start(s32[12]{0:T(128)S(1)} %copy-done.3), channel_id=1, source_target_pairs={{0,1},{1,0},{2,3},{3,2},{4,5},{5,4},{6,7},{7,6},{8,9},{9,8},{10,11... | collective-permute-start | bytes 152 | tf_op jit(solution)/shard_map/ppermute | solution.py:122
  8.9 4.8 %copy-start.4 = (s32[12]{0:T(128)}, s32[12]{0:T(128)S(1)}, u32[]{:S(2)}) copy-start(s32[12]{0:T(128)S(1)} %collective-permute-done.refs_2_) | copy-start | bytes 148
  8.9 43.3 %collective-permute-start.6 = (bf16[8,256,256]{2,1,0:T(8,128)(2,1)S(1)}, bf16[8,256,256]{2,1,0:T(8,128)(2,1)}, u32[]{:S(2)}, u32[]{:S(2)}) collective-permute-start(bf16[8,256,256]{2,1,0:T(8,128)(2,1)S(1)} %get-tuple-element.30.refs_4_), channel_id=1, source_target_pairs={{1,3},{3,5},{5,7},{7,9},{9,11},{11,13},{13,15},{2,0},{4,2},{6,4},{... | collective-permute-start | bytes 3145736 | tf_op jit(solution)/shard_map/ppermute | solution.py:117
  12.7 1.0 %copy-start.2 = (bf16[8,256,256]{2,1,0:T(8,128)(2,1)}, bf16[8,256,256]{2,1,0:T(8,128)(2,1)S(1)}, u32[]{:S(2)}) copy-start(bf16[8,256,256]{2,1,0:T(8,128)(2,1)S(1)} %collective-permute-done.2.refs_5_) | copy-start | bytes 3145732
  27.9 1.0 %copy-start.1 = (bf16[8,256,256]{2,1,0:T(8,128)(2,1)}, bf16[8,256,256]{2,1,0:T(8,128)(2,1)S(1)}, u32[]{:S(2)}) copy-start(bf16[8,256,256]{2,1,0:T(8,128)(2,1)S(1)} %collective-permute-done.5.refs_4_) | copy-start | bytes 3145732
  65.0 2.9 %collective-permute-start.7 = (bf16[8,256,256]{2,1,0:T(8,128)(2,1)}, bf16[8,256,256]{2,1,0:T(8,128)(2,1)S(1)}, u32[]{:S(2)}, u32[]{:S(2)}) collective-permute-start(bf16[8,256,256]{2,1,0:T(8,128)(2,1)} %bitcast.9), channel_id=1, source_target_pairs={{0,1},{1,0},{2,3},{3,2},{4,5},{5,4},{6,7},{7,6},{8,9},{9,8},{10,11... | collective-permute-start | bytes 3145736 | tf_op jit(solution)/shard_map/ppermute | solution.py:133
where the time goes:
time: 70.1 us; the launch traced here: 69 us
  Pallas kernels  35.6 us (51%)
  waiting for transfers between devices  20.1 us (29%)
  starting transfers between devices  7.84 us (11%)
  local copies, waits for them, and re-layouts  4.69 us (7%)
  between operations  0.72 us (1%)
    pallas_call x3, Pallas kernels, apply_pairs(): pl.pallas_call(functools.partial(pairs_kernel, phase, len(sources)), out_...  35.6 us
    ppermute x1, waiting for transfers between devices, on_device(): from_far = lax.ppermute(mine, 'sector', far)  14.7 us
    ppermute x1, starting transfers between devices, on_device(): from_far = lax.ppermute(mine, 'sector', far)  3.14 us
    ppermute x1, starting transfers between devices, on_device(): from_near = lax.ppermute(other, 'sector', near)  3.05 us
    ppermute x1, waiting for transfers between devices, on_device(): lax.ppermute(partner_half.reshape((half,) + own.shape[1:]), 'sector', par...  2.87 us
    unnamed x10, local copies, waits for them, and re-layouts  1.96 us
    dynamic_slice x1, local copies, waits for them, and re-layouts, on_device(): other = lax.dynamic_slice_in_dim(own, (1 - parity) * half, half, 0)  1.69 us
    ppermute x1, waiting for transfers between devices, on_device(): counts_p = lax.ppermute(counts, 'sector', partner)  1.64 us
  transfers between devices with their start and end apart: 8, of which 4 were waited for; matrix products, arithmetic and copies ran while one was open for 2% of the time, Pallas kernels for 33%

commit v1 on v0

--- a/solution.py
+++ b/solution.py
@@ -113,14 +113,16 @@
     far = [(j, j + 2) for j in odd if j + 2 < n] + [(j, j - 2) for j in even if j >= 2]
     partner = [(j, j ^ 1) for j in range(n)]
 
+    from_far = lax.ppermute(mine, "sector", far)
     from_near = lax.ppermute(other, "sector", near)
-    from_far = lax.ppermute(mine, "sector", far)
-    from_partner = lax.ppermute(other, "sector", partner)
-
-    left_p = lax.ppermute(left_ops, "sector", partner)
-    right_p = lax.ppermute(right_ops, "sector", partner)
-    deltas_p = lax.ppermute(deltas, "sector", partner)
-    counts_p = lax.ppermute(counts, "sector", partner)
+    slots = left_ops.shape[0]
+    packed = jnp.concatenate([other, left_ops, right_ops], 0)
+    packed = lax.ppermute(packed, "sector", partner)
+    from_partner = packed[:half]
+    left_p = packed[half:half + slots]
+    right_p = packed[half + slots:]
+    ints = lax.ppermute(jnp.concatenate([deltas, counts]), "sector", partner)
+    deltas_p, counts_p = ints[:slots], ints[slots:]
     own_job = (left_ops, right_ops, deltas, counts)
     partner_job = (left_p, right_p, deltas_p, counts_p)
 

time: 70.1 us -> 71.6 us (1.021)
  the two profiles are of different devices: /device:TPU:7 before, /device:TPU:9 now
where the time goes in v1:
time: 71.6 us; the launch traced here: 72.8 us
  Pallas kernels  34.6 us (48%)
  waiting for transfers between devices  18.2 us (25%)
  local copies, waits for them, and re-layouts  9.48 us (13%)
  starting transfers between devices  9.27 us (13%)
    pallas_call x3, Pallas kernels, apply_pairs(): pl.pallas_call(functools.partial(pairs_kernel, phase, len(sources)), out_...  34.6 us
    ppermute x1, waiting for transfers between devices, on_device(): from_near = lax.ppermute(other, 'sector', near)  14.5 us
    ppermute x1, starting transfers between devices, on_device(): from_far = lax.ppermute(mine, 'sector', far)  3.15 us
    ppermute x1, starting transfers between devices, on_device(): from_near = lax.ppermute(other, 'sector', near)  3.05 us
    dynamic_slice x1, local copies, waits for them, and re-layouts, on_device(): other = lax.dynamic_slice_in_dim(own, (1 - parity) * half, half, 0)  2.82 us
    ppermute x1, waiting for transfers between devices, on_device(): lax.ppermute(partner_half.reshape((half,) + own.shape[1:]), 'sector', par...  2.5 us
    ppermute x1, starting transfers between devices, on_device(): lax.ppermute(partner_half.reshape((half,) + own.shape[1:]), 'sector', par...  2.33 us
    slice x1, local copies, waits for them, and re-layouts, on_device(): right_p = packed[half + slots:]  2.01 us
  transfers between devices with their start and end apart: 5, of which 3 were waited for; matrix products, arithmetic and copies ran while one was open for 5% of the time, Pallas kernels for 36%

profile of v1, /device:TPU:9, one launch (start us, length us, event | category | flops | bytes accessed | tf_op | source)
XLA Modules:
  0.0 72.8 jit_solution(4351716541006956071)
XLA Ops:
  0.0 2.8 %dynamic-slice_bitcast_fusion = (bf16[8,256,256]{2,1,0:T(8,128)(2,1)S(1)}, bf16[8,256,256]{2,1,0:T(8,128)(2,1)}) fusion(bf16[1,16,256,256]{3,2,1,0:T(8,128)(2,1)} %param.5, s32[]{:T(128)S(6)} %select_n.16, s32[]{:T(128)S(6)} %select_n.15), kind=kLoop, calls=%fused_computation.2 | loop fusion | bytes 4194312 | tf_op jit(solution)/shard_map/dynamic_slice | solution.py:109
  2.8 0.0 copy-done
  2.8 0.5 pad_maximum_fusion
  3.3 0.7 %collective-permute-start.1 = (bf16[32,256,256]{2,1,0:T(8,128)(2,1)S(1)}, bf16[32,256,256]{2,1,0:T(8,128)(2,1)S(1)}, u32[]{:S(2)}, u32[]{:S(2)}) collective-permute-start(bf16[32,256,256]{2,1,0:T(8,128)(2,1)S(1)} %pad_maximum_fusion), channel_id=1, source_target_pairs={{0,1},{1,0},{2,3},{3,2},{4,5},{5,4},{6,7},{7,6},{8,9},{9,8},{10,11... | collective-permute-start | bytes 12582920 | tf_op jit(solution)/shard_map/ppermute | solution.py:120
  4.1 3.0 %collective-permute-start.2 = (bf16[8,256,256]{2,1,0:T(8,128)(2,1)S(1)}, bf16[8,256,256]{2,1,0:T(8,128)(2,1)S(1)}, u32[]{:S(2)}, u32[]{:S(2)}) collective-permute-start(bf16[8,256,256]{2,1,0:T(8,128)(2,1)S(1)} %get-tuple-element.31), channel_id=1, source_target_pairs={{1,2},{3,4},{5,6},{7,8},{9,10},{11,12},{13,14},{2,1},{4,3},{6,5},{... | collective-permute-start | bytes 3145736 | tf_op jit(solution)/shard_map/ppermute | solution.py:117
  7.1 3.1 %collective-permute-start.3 = (bf16[8,256,256]{2,1,0:T(8,128)(2,1)}, bf16[8,256,256]{2,1,0:T(8,128)(2,1)S(1)}, u32[]{:S(2)}, u32[]{:S(2)}) collective-permute-start(bf16[8,256,256]{2,1,0:T(8,128)(2,1)} %get-tuple-element.32.refs_4_), channel_id=1, source_target_pairs={{1,3},{3,5},{5,7},{7,9},{9,11},{11,13},{13,15},{2,0},{4,2},{6,4},{... | collective-permute-start | bytes 3145736 | tf_op jit(solution)/shard_map/ppermute | solution.py:116
  10.9 0.1 pad_add_fusion
  11.0 0.0 collective-permute-start
  11.0 1.1 %collective-permute-done = s32[13]{0:T(128)S(1)} collective-permute-done((s32[13]{0:T(128)S(1)}, s32[13]{0:T(128)S(1)}, u32[]{:S(2)}, u32[]{:S(2)}) %collective-permute-start) | collective-permute-done | bytes 84 | tf_op jit(solution)/shard_map/ppermute | solution.py:124
  12.1 0.6 slice.16.refs_3_
  12.7 0.0 collective-permute-done.1
  12.8 1.0 %slice.20.refs_5_ = bf16[8,256,256]{2,1,0:T(8,128)(2,1)} slice(bf16[32,256,256]{2,1,0:T(8,128)(2,1)S(1)} %collective-permute-done.1), slice={[0:8], [0:256], [0:256]} | slice | bytes 2097152 | tf_op jit(solution)/shard_map/slice | solution.py:121
  13.8 2.0 %fusion = (bf16[12,256,256]{2,1,0:T(8,128)(2,1)}, bf16[12,256,256]{2,1,0:T(8,128)(2,1)}) fusion(bf16[32,256,256]{2,1,0:T(8,128)(2,1)S(1)} %collective-permute-done.1), kind=kLoop, calls=%fused_computation.5 | loop fusion | bytes 6291456 | tf_op jit(solution)/shard_map/slice | solution.py:123
  15.8 0.0 copy-done.5
  15.8 12.3 %shard_map.55 = (f32[2048,256]{1,0:T(8,128)}, f32[2048,256]{1,0:T(8,128)}) custom-call(s32[12]{0:T(128)} %refs_0_.5, s32[1]{0:T(128)S(6)} %copy.7.refs_1_, s32[12]{0:T(128)} %bitcast.11, s32[1]{0:T(128)} %slice.16.refs_3_, bf16[8,256,256]{2,1,0:T(8,128)(2,1)} %get-tuple-element.32.refs_4_, bf16[8,256,256]{2,1,0:T(8,128)(2,1)} %slice.20.refs_5_, ...), custom_call_target="tpu_custom_call" | custom-call | flops 3221225472 | bytes 16777216 | tf_op jit(solution)/shard_map/pallas_call | solution.py:89
  28.1 14.5 %collective-permute-done.2.refs_4_ = bf16[8,256,256]{2,1,0:T(8,128)(2,1)S(1)} collective-permute-done((bf16[8,256,256]{2,1,0:T(8,128)(2,1)S(1)}, bf16[8,256,256]{2,1,0:T(8,128)(2,1)S(1)}, u32[]{:S(2)}, u32[]{:S(2)}) %collective-permute-start.2) | collective-permute-done | bytes 1048608 | tf_op jit(solution)/shard_map/ppermute | solution.py:117
  42.7 1.0 %copy-done.3 = bf16[8,256,256]{2,1,0:T(8,128)(2,1)} copy-done((bf16[8,256,256]{2,1,0:T(8,128)(2,1)}, bf16[8,256,256]{2,1,0:T(8,128)(2,1)S(1)}, u32[]{:S(2)}) %copy-start.3) | copy-done | bytes 1048600
  43.6 14.0 %shard_map.56 = (f32[2048,256]{1,0:T(8,128)}, f32[2048,256]{1,0:T(8,128)}) custom-call(s32[12]{0:T(128)} %refs_0_.5, s32[1]{0:T(128)S(6)} %copy.7.refs_1_, s32[12]{0:T(128)} %bitcast.12, s32[1]{0:T(128)} %slice.16.refs_3_, bf16[8,256,256]{2,1,0:T(8,128)(2,1)} %copy-done.3, bf16[12,256,256]{2,1,0:T(8,128)(2,1)} %refs_5_.3, bf16[12,256,256]{2,1,0:T(8,128)(2,1)} %refs_6_.5, ...), custom_call_target="tpu_custom_call" | custom-call | flops 3221225472 | bytes 15728640 | tf_op jit(solution)/shard_map/pallas_call | solution.py:89
  57.7 0.0 collective-permute-done.3.refs_4_
  57.7 1.0 %copy-done.2 = bf16[8,256,256]{2,1,0:T(8,128)(2,1)} copy-done((bf16[8,256,256]{2,1,0:T(8,128)(2,1)}, bf16[8,256,256]{2,1,0:T(8,128)(2,1)S(1)}, u32[]{:S(2)}) %copy-start.2) | copy-done | bytes 1048600
  58.6 8.3 %shard_map.57 = (bf16[4096,256]{1,0:T(8,128)(2,1)}, bf16[2048,256]{1,0:T(8,128)(2,1)}) custom-call(s32[12]{0:T(128)} %refs_0_.5, s32[1]{0:T(128)S(6)} %copy.7.refs_1_, s32[12]{0:T(128)} %bitcast.13, s32[1]{0:T(128)} %slice.16.refs_3_, bf16[8,256,256]{2,1,0:T(8,128)(2,1)} %copy-done.2, bf16[12,256,256]{2,1,0:T(8,128)(2,1)} %refs_5_.3, ...), custom_call_target="tpu_custom_call" | custom-call | flops 3221225472 | bytes 15728640 | tf_op jit(solution)/shard_map/pallas_call | solution.py:89
  66.9 2.3 %collective-permute-start.4 = (bf16[8,256,256]{2,1,0:T(8,128)(2,1)}, bf16[8,256,256]{2,1,0:T(8,128)(2,1)S(1)}, u32[]{:S(2)}, u32[]{:S(2)}) collective-permute-start(bf16[8,256,256]{2,1,0:T(8,128)(2,1)} %bitcast.10), channel_id=1, source_target_pairs={{0,1},{1,0},{2,3},{3,2},{4,5},{5,4},{6,7},{7,6},{8,9},{9,8},{10,11... | collective-permute-start | bytes 3145736 | tf_op jit(solution)/shard_map/ppermute | solution.py:135
  69.3 2.5 %collective-permute-done.4 = bf16[8,256,256]{2,1,0:T(8,128)(2,1)S(1)} collective-permute-done((bf16[8,256,256]{2,1,0:T(8,128)(2,1)}, bf16[8,256,256]{2,1,0:T(8,128)(2,1)S(1)}, u32[]{:S(2)}, u32[]{:S(2)}) %collective-permute-start.4) | collective-permute-done | bytes 1048608 | tf_op jit(solution)/shard_map/ppermute | solution.py:135
  71.8 1.0 %bitcast_dynamic-update-slice_fusion = bf16[1,16,256,256]{3,2,1,0:T(8,128)(2,1)} fusion(bf16[1,16,256,256]{3,2,1,0:T(8,128)(2,1)} %bitcast.9, s32[]{:T(128)S(6)} %select_n.16, bf16[8,256,256]{2,1,0:T(8,128)(2,1)S(1)} %collective-permute-done.4), kind=kLoop, calls=%fused_computation.1 | loop fusion | bytes 2097156 | tf_op jit(solution)/shard_map/dynamic_update_slice | solution.py:136
  (8 shorter events, 0.0 us)
Async XLA Ops:
  0.0 2.8 %copy-start = (bf16[12,256,256]{2,1,0:T(8,128)(2,1)S(1)}, bf16[12,256,256]{2,1,0:T(8,128)(2,1)}, u32[]{:S(2)}) copy-start(bf16[12,256,256]{2,1,0:T(8,128)(2,1)} %refs_5_.3) | copy-start | bytes 4718596
  0.0 2.8 %copy-start.1 = (bf16[12,256,256]{2,1,0:T(8,128)(2,1)S(1)}, bf16[12,256,256]{2,1,0:T(8,128)(2,1)}, u32[]{:S(2)}) copy-start(bf16[12,256,256]{2,1,0:T(8,128)(2,1)} %refs_6_.5) | copy-start | bytes 4718596
  2.8 8.1 %copy-start.4 = (s32[12]{0:T(128)S(1)}, s32[12]{0:T(128)}, u32[]{:S(2)}) copy-start(s32[12]{0:T(128)} %refs_0_.5) | copy-start | bytes 148
  3.3 9.4 %collective-permute-start.1 = (bf16[32,256,256]{2,1,0:T(8,128)(2,1)S(1)}, bf16[32,256,256]{2,1,0:T(8,128)(2,1)S(1)}, u32[]{:S(2)}, u32[]{:S(2)}) collective-permute-start(bf16[32,256,256]{2,1,0:T(8,128)(2,1)S(1)} %pad_maximum_fusion), channel_id=1, source_target_pairs={{0,1},{1,0},{2,3},{3,2},{4,5},{5,4},{6,7},{7,6},{8,9},{9,8},{10,11... | collective-permute-start | bytes 12582920 | tf_op jit(solution)/shard_map/ppermute | solution.py:120
  4.1 38.6 %collective-permute-start.2 = (bf16[8,256,256]{2,1,0:T(8,128)(2,1)S(1)}, bf16[8,256,256]{2,1,0:T(8,128)(2,1)S(1)}, u32[]{:S(2)}, u32[]{:S(2)}) collective-permute-start(bf16[8,256,256]{2,1,0:T(8,128)(2,1)S(1)} %get-tuple-element.31), channel_id=1, source_target_pairs={{1,2},{3,4},{5,6},{7,8},{9,10},{11,12},{13,14},{2,1},{4,3},{6,5},{... | collective-permute-start | bytes 3145736 | tf_op jit(solution)/shard_map/ppermute | solution.py:117
  7.1 50.5 %collective-permute-start.3 = (bf16[8,256,256]{2,1,0:T(8,128)(2,1)}, bf16[8,256,256]{2,1,0:T(8,128)(2,1)S(1)}, u32[]{:S(2)}, u32[]{:S(2)}) collective-permute-start(bf16[8,256,256]{2,1,0:T(8,128)(2,1)} %get-tuple-element.32.refs_4_), channel_id=1, source_target_pairs={{1,3},{3,5},{5,7},{7,9},{9,11},{11,13},{13,15},{2,0},{4,2},{6,4},{... | collective-permute-start | bytes 3145736 | tf_op jit(solution)/shard_map/ppermute | solution.py:116
  11.0 1.1 %collective-permute-start = (s32[13]{0:T(128)S(1)}, s32[13]{0:T(128)S(1)}, u32[]{:S(2)}, u32[]{:S(2)}) collective-permute-start(s32[13]{0:T(128)S(1)} %pad_add_fusion), channel_id=1, source_target_pairs={{0,1},{1,0},{2,3},{3,2},{4,5},{5,4},{6,7},{7,6},{8,9},{9,8},{10,11... | collective-permute-start | bytes 164 | tf_op jit(solution)/shard_map/ppermute | solution.py:124
  12.1 3.7 %copy-start.5 = (s32[13]{0:T(128)}, s32[13]{0:T(128)S(1)}, u32[]{:S(2)}) copy-start(s32[13]{0:T(128)S(1)} %collective-permute-done) | copy-start | bytes 160
  42.7 1.0 %copy-start.3 = (bf16[8,256,256]{2,1,0:T(8,128)(2,1)}, bf16[8,256,256]{2,1,0:T(8,128)(2,1)S(1)}, u32[]{:S(2)}) copy-start(bf16[8,256,256]{2,1,0:T(8,128)(2,1)S(1)} %collective-permute-done.2.refs_4_) | copy-start | bytes 3145732
  57.7 1.0 %copy-start.2 = (bf16[8,256,256]{2,1,0:T(8,128)(2,1)}, bf16[8,256,256]{2,1,0:T(8,128)(2,1)S(1)}, u32[]{:S(2)}) copy-start(bf16[8,256,256]{2,1,0:T(8,128)(2,1)S(1)} %collective-permute-done.3.refs_4_) | copy-start | bytes 3145732
  66.9 4.8 %collective-permute-start.4 = (bf16[8,256,256]{2,1,0:T(8,128)(2,1)}, bf16[8,256,256]{2,1,0:T(8,128)(2,1)S(1)}, u32[]{:S(2)}, u32[]{:S(2)}) collective-permute-start(bf16[8,256,256]{2,1,0:T(8,128)(2,1)} %bitcast.10), channel_id=1, source_target_pairs={{0,1},{1,0},{2,3},{3,2},{4,5},{5,4},{6,7},{7,6},{8,9},{9,8},{10,11... | collective-permute-start | bytes 3145736 | tf_op jit(solution)/shard_map/ppermute | solution.py:135

commit v2 on v0

--- a/solution.py
+++ b/solution.py
@@ -16,25 +16,22 @@
     return jnp.where(phys == phase, 0, 2)
 
 
-def pairs_kernel(phase, n_src, *refs):
-    d_own, c_own, d_par, c_par = refs[:4]
-    srcs = refs[4:4 + n_src]
-    l_own, r_own, l_par, r_par = refs[4 + n_src:8 + n_src]
-    rest = refs[8 + n_src:]
-    if phase > 0:
-        s_own, s_par = rest[:2]
-        rest = rest[2:]
-    else:
-        s_own = s_par = None
-    o_own, o_par, acc_ref, mixed_ref = rest
+def pairs_kernel(phase, jobs, n_src, *refs):
+    njobs = len(jobs)
+    ints = refs[:2 * njobs]
+    srcs = refs[2 * njobs:2 * njobs + n_src]
+    ops = refs[2 * njobs + n_src:4 * njobs + n_src]
+    rest = refs[4 * njobs + n_src:]
+    starts = rest[:njobs] if phase > 0 else (None,) * njobs
+    rest = rest[njobs:] if phase > 0 else rest
+    outs, (acc_ref, mixed_ref) = rest[:njobs], rest[njobs:]
     rows, width = srcs[0].shape[0], srcs[0].shape[1]
     size = rows * width
     parity = lax.axis_index("sector") % 2
-    jobs = (
-        (False, d_par, c_par, l_par, r_par, s_par, o_par),
-        (True, d_own, c_own, l_own, r_own, s_own, o_own),
-    )
-    for mine_first, deltas_ref, count_ref, left_ref, right_ref, start_ref, out_ref in jobs:
+    for j, mine_first in enumerate(jobs):
+        deltas_ref, count_ref = ints[2 * j], ints[2 * j + 1]
+        left_ref, right_ref = ops[2 * j], ops[2 * j + 1]
+        start_ref, out_ref = starts[j], outs[j]
         if start_ref is None:
             acc_ref[...] = jnp.zeros_like(acc_ref)
         else:
@@ -62,41 +59,40 @@
             return carry
 
         lax.fori_loop(0, jnp.minimum(count_ref[0], left_ref.shape[0]), step, 0)
-        if phase == 2 and mine_first:
+        if phase > 0 and mine_first:
             offset = pl.multiple_of(parity * size, size)
             out_ref[pl.ds(offset, size), :] = acc_ref[...].astype(out_ref.dtype)
         else:
             out_ref[...] = acc_ref[...].astype(out_ref.dtype)
 
 
-def apply_pairs(phase, sources, own_job, partner_job, starts=()):
+def apply_pairs(phase, sources, jobs, starts=()):
     rows, width = sources[0].shape[0], sources[0].shape[1]
     size = rows * width
-    left_ops, right_ops, deltas, counts = own_job
-    left_p, right_p, deltas_p, counts_p = partner_job
-    slots = left_ops.shape[0]
+    slots = jobs[0][1][0].shape[0]
     vmem = pl.BlockSpec(memory_space=pltpu.VMEM)
     smem = pl.BlockSpec(memory_space=pltpu.SMEM)
-    flops = 4 * slots * size * width * width // 2
-    moved = 2 * (len(sources) * size * width + 4 * slots * width * width) + 16 * size * width
-    if phase == 2:
-        outs = (
-            jax.ShapeDtypeStruct((2 * size, width), jnp.bfloat16),
-            jax.ShapeDtypeStruct((size, width), jnp.bfloat16),
-        )
-    else:
-        outs = (jax.ShapeDtypeStruct((size, width), jnp.float32),) * 2
+    flops = 2 * slots * size * width * width * len(jobs) // 3
+    moved = 2 * (len(sources) * size * width + 2 * len(jobs) * slots * width * width) + 8 * len(jobs) * size * width
+    outs = []
+    for is_own, _ in jobs:
+        if phase == 0:
+            outs.append(jax.ShapeDtypeStruct((size, width), jnp.float32))
+        else:
+            outs.append(jax.ShapeDtypeStruct(((2 if is_own else 1) * size, width), jnp.bfloat16))
+    ints = [x for _, (l, r, d, c) in jobs for x in (d, c)]
+    ops = [x for _, (l, r, d, c) in jobs for x in (l, r)]
     return pl.pallas_call(
-        functools.partial(pairs_kernel, phase, len(sources)),
-        out_shape=outs,
-        in_specs=[smem] * 4 + [vmem] * (len(sources) + 4 + len(starts)),
-        out_specs=(vmem, vmem),
+        functools.partial(pairs_kernel, phase, tuple(o for o, _ in jobs), len(sources)),
+        out_shape=tuple(outs),
+        in_specs=[smem] * len(ints) + [vmem] * (len(sources) + len(ops) + len(starts)),
+        out_specs=tuple(vmem for _ in outs),
         scratch_shapes=[
             pltpu.VMEM((size, width), jnp.float32),
             pltpu.VMEM((size, width), jnp.bfloat16),
         ],
         cost_estimate=pl.CostEstimate(flops=flops, bytes_accessed=moved, transcendentals=0),
-    )(deltas, counts, deltas_p, counts_p, *sources, left_ops, right_ops, left_p, right_p, *starts)
+    )(*ints, *sources, *ops, *starts)
 
 
 def on_device(wave, left_ops, right_ops, deltas, counts):
@@ -124,11 +120,11 @@
     own_job = (left_ops, right_ops, deltas, counts)
     partner_job = (left_p, right_p, deltas_p, counts_p)
 
-    own_sum, partner_sum = apply_pairs(0, (mine, from_partner), own_job, partner_job)
+    partner_sum, own_sum = apply_pairs(0, (mine, from_partner), ((False, partner_job), (True, own_job)))
     own_sum, partner_sum, from_near = lax.optimization_barrier((own_sum, partner_sum, from_near))
-    own_sum, partner_sum = apply_pairs(1, (from_near,), own_job, partner_job, (own_sum, partner_sum))
-    own_sum, partner_sum, from_far = lax.optimization_barrier((own_sum, partner_sum, from_far))
-    out, partner_half = apply_pairs(2, (from_far,), own_job, partner_job, (own_sum, partner_sum))
+    (out,) = apply_pairs(1, (from_near,), ((True, own_job),), (own_sum,))
+    out, partner_sum, from_far = lax.optimization_barrier((out, partner_sum, from_far))
+    (partner_half,) = apply_pairs(2, (from_far,), ((False, partner_job),), (partner_sum,))
 
     returned = lax.ppermute(partner_half.reshape((half,) + own.shape[1:]), "sector", partner)
     out = lax.dynamic_update_slice_in_dim(out.reshape(own.shape), returned, (1 - parity) * half, 0)

time: 70.1 us -> 69.3 us (0.989)
  the two profiles are of different devices: /device:TPU:7 before, /device:TPU:19 now
where the time goes in v2:
time: 69.3 us; the launch traced here: 70 us
  Pallas kernels  29 us (42%)
  waiting for transfers between devices  18.3 us (26%)
  starting transfers between devices  14.5 us (21%)
  local copies, waits for them, and re-layouts  7.47 us (11%)
  between operations  0.7 us (1%)
    pallas_call x3, Pallas kernels, apply_pairs(): pl.pallas_call(functools.partial(pairs_kernel, phase, tuple((o for o, _ i...  29 us
    ppermute x1, waiting for transfers between devices, on_device(): from_near = lax.ppermute(other, 'sector', near)  14 us
    ppermute x1, starting transfers between devices, on_device(): lax.ppermute(partner_half.reshape((half,) + own.shape[1:]), 'sector', par...  6.53 us
    unnamed x10, local copies, waits for them, and re-layouts  3.34 us
    dynamic_slice x1, local copies, waits for them, and re-layouts, on_device(): other = lax.dynamic_slice_in_dim(own, (1 - parity) * half, half, 0)  3.1 us
    ppermute x1, starting transfers between devices, on_device(): from_far = lax.ppermute(mine, 'sector', far)  3.03 us
    ppermute x1, starting transfers between devices, on_device(): from_near = lax.ppermute(other, 'sector', near)  3.03 us
    ppermute x1, waiting for transfers between devices, on_device(): lax.ppermute(partner_half.reshape((half,) + own.shape[1:]), 'sector', par...  2.5 us
  transfers between devices with their start and end apart: 8, of which 4 were waited for; matrix products, arithmetic and copies ran while one was open for 4% of the time, Pallas kernels for 33%

profile of v2, /device:TPU:19, one launch (start us, length us, event | category | flops | bytes accessed | tf_op | source)
XLA Modules:
  0.0 70.0 jit_solution(4720515382076839628)
XLA Ops:
  0.0 0.7 collective-permute-start.3
  0.7 0.0 collective-permute-start.4
  0.7 3.1 %dynamic-slice_bitcast_fusion = (bf16[8,256,256]{2,1,0:T(8,128)(2,1)}, bf16[8,256,256]{2,1,0:T(8,128)(2,1)}) fusion(bf16[1,16,256,256]{3,2,1,0:T(8,128)(2,1)} %param.5, s32[]{:T(128)S(6)} %select_n.16, s32[]{:T(128)S(6)} %select_n.15), kind=kLoop, calls=%fused_computation.1 | loop fusion | bytes 4194312 | tf_op jit(solution)/shard_map/dynamic_slice | solution.py:105
  3.8 0.5 collective-permute-start.2
  4.3 3.0 %collective-permute-start.5 = (bf16[8,256,256]{2,1,0:T(8,128)(2,1)}, bf16[8,256,256]{2,1,0:T(8,128)(2,1)}, u32[]{:S(2)}, u32[]{:S(2)}) collective-permute-start(bf16[8,256,256]{2,1,0:T(8,128)(2,1)} %get-tuple-element.21), channel_id=1, source_target_pairs={{1,2},{3,4},{5,6},{7,8},{9,10},{11,12},{13,14},{2,1},{4,3},{6,5},{... | collective-permute-start | bytes 3145736 | tf_op jit(solution)/shard_map/ppermute | solution.py:112
  7.3 0.5 collective-permute-start.1
  7.8 1.0 %collective-permute-done.1.refs_1_ = s32[1]{0:T(128)} collective-permute-done((s32[1]{0:T(128)}, s32[1]{0:T(128)}, u32[]{:S(2)}, u32[]{:S(2)}) %collective-permute-start.1) | collective-permute-done | bytes 36 | tf_op jit(solution)/shard_map/ppermute | solution.py:119
  8.7 0.3 collective-permute-start
  9.0 0.8 %collective-permute-done.refs_0_ = s32[12]{0:T(128)S(1)} collective-permute-done((s32[12]{0:T(128)S(1)}, s32[12]{0:T(128)S(1)}, u32[]{:S(2)}, u32[]{:S(2)}) %collective-permute-start) | collective-permute-done | bytes 80 | tf_op jit(solution)/shard_map/ppermute | solution.py:118
  9.9 3.0 %collective-permute-start.6 = (bf16[8,256,256]{2,1,0:T(8,128)(2,1)}, bf16[8,256,256]{2,1,0:T(8,128)(2,1)}, u32[]{:S(2)}, u32[]{:S(2)}) collective-permute-start(bf16[8,256,256]{2,1,0:T(8,128)(2,1)} %get-tuple-element.22.refs_4_), channel_id=1, source_target_pairs={{1,3},{3,5},{5,7},{7,9},{9,11},{11,13},{13,15},{2,0},{4,2},{6,4},{... | collective-permute-start | bytes 3145736 | tf_op jit(solution)/shard_map/ppermute | solution.py:113
  13.5 0.0 collective-permute-done.2.refs_5_
  13.6 0.0 collective-permute-done.3.refs_6_.refs_3_
  13.6 1.0 %copy-done.2 = bf16[8,256,256]{2,1,0:T(8,128)(2,1)} copy-done((bf16[8,256,256]{2,1,0:T(8,128)(2,1)}, bf16[8,256,256]{2,1,0:T(8,128)(2,1)S(1)}, u32[]{:S(2)}) %copy-start.2) | copy-done | bytes 1048600
  14.5 0.0 collective-permute-done.4.refs_7_.refs_4_
  14.6 1.2 %copy-done = bf16[12,256,256]{2,1,0:T(8,128)(2,1)} copy-done((bf16[12,256,256]{2,1,0:T(8,128)(2,1)}, bf16[12,256,256]{2,1,0:T(8,128)(2,1)S(1)}, u32[]{:S(2)}) %copy-start) | copy-done | bytes 1572888
  15.7 1.2 %copy-done.1 = bf16[12,256,256]{2,1,0:T(8,128)(2,1)} copy-done((bf16[12,256,256]{2,1,0:T(8,128)(2,1)}, bf16[12,256,256]{2,1,0:T(8,128)(2,1)S(1)}, u32[]{:S(2)}) %copy-start.1) | copy-done | bytes 1572888
  16.9 12.2 %shard_map.55 = (f32[2048,256]{1,0:T(8,128)}, f32[2048,256]{1,0:T(8,128)}) custom-call(s32[12]{0:T(128)} %copy-done.4, s32[1]{0:T(128)} %collective-permute-done.1.refs_1_, s32[12]{0:T(128)} %refs_0_.1, s32[1]{0:T(128)S(6)} %copy.7.refs_3_.refs_1_, bf16[8,256,256]{2,1,0:T(8,128)(2,1)} %get-tuple-element.22.refs_4_, bf16[8,256,256]{2,1,0:T(8,128)(2,1)} %copy-done.2, ...), custom_call_target="tpu_custom_call" | custom-call | flops 2147483648 | bytes 16777216 | tf_op jit(solution)/shard_map/pallas_call | solution.py:85
  29.1 14.0 %collective-permute-done.5.refs_2_ = bf16[8,256,256]{2,1,0:T(8,128)(2,1)} collective-permute-done((bf16[8,256,256]{2,1,0:T(8,128)(2,1)}, bf16[8,256,256]{2,1,0:T(8,128)(2,1)}, u32[]{:S(2)}, u32[]{:S(2)}) %collective-permute-start.5) | collective-permute-done | bytes 1048608 | tf_op jit(solution)/shard_map/ppermute | solution.py:112
  43.2 11.0 %shard_map.56 = bf16[4096,256]{1,0:T(8,128)(2,1)} custom-call(s32[12]{0:T(128)} %refs_0_.1, s32[1]{0:T(128)S(6)} %copy.7.refs_3_.refs_1_, bf16[8,256,256]{2,1,0:T(8,128)(2,1)} %collective-permute-done.5.refs_2_, bf16[12,256,256]{2,1,0:T(8,128)(2,1)} %refs_3_.2, bf16[12,256,256]{2,1,0:T(8,128)(2,1)} %refs_4_.1, f32[2048,256]{1,0:T(8,128)} %get-tuple-element.16.refs_5_), custom_call_target="tpu_custom_call" | custom-call | flops 1073741824 | bytes 8388608 | tf_op jit(solution)/shard_map/pallas_call | solution.py:85
  54.2 0.0 collective-permute-done.6.refs_2_
  54.2 5.7 %shard_map.57 = bf16[2048,256]{1,0:T(8,128)(2,1)} custom-call(s32[12]{0:T(128)} %copy-done.4, s32[1]{0:T(128)} %collective-permute-done.1.refs_1_, bf16[8,256,256]{2,1,0:T(8,128)(2,1)} %collective-permute-done.6.refs_2_, bf16[12,256,256]{2,1,0:T(8,128)(2,1)} %copy-done, bf16[12,256,256]{2,1,0:T(8,128)(2,1)} %copy-done.1, f32[2048,256]{1,0:T(8,128)} %get-tuple-element.20.refs_5_), custom_call_target="tpu_custom_call" | custom-call | flops 1073741824 | bytes 8388608 | tf_op jit(solution)/shard_map/pallas_call | solution.py:85
  59.9 6.5 %collective-permute-start.7 = (bf16[8,256,256]{2,1,0:T(8,128)(2,1)}, bf16[8,256,256]{2,1,0:T(8,128)(2,1)S(1)}, u32[]{:S(2)}, u32[]{:S(2)}) collective-permute-start(bf16[8,256,256]{2,1,0:T(8,128)(2,1)} %bitcast.9), channel_id=1, source_target_pairs={{0,1},{1,0},{2,3},{3,2},{4,5},{5,4},{6,7},{7,6},{8,9},{9,8},{10,11... | collective-permute-start | bytes 3145736 | tf_op jit(solution)/shard_map/ppermute | solution.py:129
  66.5 2.5 %collective-permute-done.7 = bf16[8,256,256]{2,1,0:T(8,128)(2,1)S(1)} collective-permute-done((bf16[8,256,256]{2,1,0:T(8,128)(2,1)}, bf16[8,256,256]{2,1,0:T(8,128)(2,1)S(1)}, u32[]{:S(2)}, u32[]{:S(2)}) %collective-permute-start.7) | collective-permute-done | bytes 1048608 | tf_op jit(solution)/shard_map/ppermute | solution.py:129
  69.0 1.0 %bitcast_dynamic-update-slice_fusion = bf16[1,16,256,256]{3,2,1,0:T(8,128)(2,1)} fusion(bf16[1,16,256,256]{3,2,1,0:T(8,128)(2,1)} %bitcast.8, s32[]{:T(128)S(6)} %select_n.16, bf16[8,256,256]{2,1,0:T(8,128)(2,1)S(1)} %collective-permute-done.7), kind=kLoop, calls=%fused_computation | loop fusion | bytes 2097156 | tf_op jit(solution)/shard_map/dynamic_update_slice | solution.py:130
  (7 shorter events, 0.0 us)
Async XLA Ops:
  0.0 13.6 %collective-permute-start.3 = (bf16[12,256,256]{2,1,0:T(8,128)(2,1)}, bf16[12,256,256]{2,1,0:T(8,128)(2,1)S(1)}, u32[]{:S(2)}, u32[]{:S(2)}) collective-permute-start(bf16[12,256,256]{2,1,0:T(8,128)(2,1)} %refs_3_.2), channel_id=1, source_target_pairs={{0,1},{1,0},{2,3},{3,2},{4,5},{5,4},{6,7},{7,6},{8,9},{9,8},{10,11... | collective-permute-start | bytes 4718600 | tf_op jit(solution)/shard_map/ppermute | solution.py:116
  0.7 13.9 %collective-permute-start.4 = (bf16[12,256,256]{2,1,0:T(8,128)(2,1)}, bf16[12,256,256]{2,1,0:T(8,128)(2,1)S(1)}, u32[]{:S(2)}, u32[]{:S(2)}) collective-permute-start(bf16[12,256,256]{2,1,0:T(8,128)(2,1)} %refs_4_.1), channel_id=1, source_target_pairs={{0,1},{1,0},{2,3},{3,2},{4,5},{5,4},{6,7},{7,6},{8,9},{9,8},{10,11... | collective-permute-start | bytes 4718600 | tf_op jit(solution)/shard_map/ppermute | solution.py:117
  0.7 8.1 %copy-start.3 = (s32[12]{0:T(128)S(1)}, s32[12]{0:T(128)}, u32[]{:S(2)}) copy-start(s32[12]{0:T(128)} %refs_0_.1) | copy-start | bytes 148
  3.8 9.8 %collective-permute-start.2 = (bf16[8,256,256]{2,1,0:T(8,128)(2,1)}, bf16[8,256,256]{2,1,0:T(8,128)(2,1)S(1)}, u32[]{:S(2)}, u32[]{:S(2)}) collective-permute-start(bf16[8,256,256]{2,1,0:T(8,128)(2,1)} %get-tuple-element.21), channel_id=1, source_target_pairs={{0,1},{1,0},{2,3},{3,2},{4,5},{5,4},{6,7},{7,6},{8,9},{9,8},{10,11... | collective-permute-start | bytes 3145736 | tf_op jit(solution)/shard_map/ppermute | solution.py:114
  4.3 38.9 %collective-permute-start.5 = (bf16[8,256,256]{2,1,0:T(8,128)(2,1)}, bf16[8,256,256]{2,1,0:T(8,128)(2,1)}, u32[]{:S(2)}, u32[]{:S(2)}) collective-permute-start(bf16[8,256,256]{2,1,0:T(8,128)(2,1)} %get-tuple-element.21), channel_id=1, source_target_pairs={{1,2},{3,4},{5,6},{7,8},{9,10},{11,12},{13,14},{2,1},{4,3},{6,5},{... | collective-permute-start | bytes 3145736 | tf_op jit(solution)/shard_map/ppermute | solution.py:112
  7.3 1.4 %collective-permute-start.1 = (s32[1]{0:T(128)}, s32[1]{0:T(128)}, u32[]{:S(2)}, u32[]{:S(2)}) collective-permute-start(s32[1]{0:T(128)} %param.9), channel_id=1, source_target_pairs={{0,1},{1,0},{2,3},{3,2},{4,5},{5,4},{6,7},{7,6},{8,9},{9,8},{10,11... | collective-permute-start | bytes 20 | tf_op jit(solution)/shard_map/ppermute | solution.py:119
  8.7 1.1 %collective-permute-start = (s32[12]{0:T(128)S(1)}, s32[12]{0:T(128)S(1)}, u32[]{:S(2)}, u32[]{:S(2)}) collective-permute-start(s32[12]{0:T(128)S(1)} %copy-done.3), channel_id=1, source_target_pairs={{0,1},{1,0},{2,3},{3,2},{4,5},{5,4},{6,7},{7,6},{8,9},{9,8},{10,11... | collective-permute-start | bytes 152 | tf_op jit(solution)/shard_map/ppermute | solution.py:118
  9.9 4.7 %copy-start.4 = (s32[12]{0:T(128)}, s32[12]{0:T(128)S(1)}, u32[]{:S(2)}) copy-start(s32[12]{0:T(128)S(1)} %collective-permute-done.refs_0_) | copy-start | bytes 148
  9.9 44.4 %collective-permute-start.6 = (bf16[8,256,256]{2,1,0:T(8,128)(2,1)}, bf16[8,256,256]{2,1,0:T(8,128)(2,1)}, u32[]{:S(2)}, u32[]{:S(2)}) collective-permute-start(bf16[8,256,256]{2,1,0:T(8,128)(2,1)} %get-tuple-element.22.refs_4_), channel_id=1, source_target_pairs={{1,3},{3,5},{5,7},{7,9},{9,11},{11,13},{13,15},{2,0},{4,2},{6,4},{... | collective-permute-start | bytes 3145736 | tf_op jit(solution)/shard_map/ppermute | solution.py:113
  13.6 1.0 %copy-start.2 = (bf16[8,256,256]{2,1,0:T(8,128)(2,1)}, bf16[8,256,256]{2,1,0:T(8,128)(2,1)S(1)}, u32[]{:S(2)}) copy-start(bf16[8,256,256]{2,1,0:T(8,128)(2,1)S(1)} %collective-permute-done.2.refs_5_) | copy-start | bytes 3145732
  14.5 1.2 %copy-start = (bf16[12,256,256]{2,1,0:T(8,128)(2,1)}, bf16[12,256,256]{2,1,0:T(8,128)(2,1)S(1)}, u32[]{:S(2)}) copy-start(bf16[12,256,256]{2,1,0:T(8,128)(2,1)S(1)} %collective-permute-done.3.refs_6_.refs_3_) | copy-start | bytes 4718596
  15.7 1.2 %copy-start.1 = (bf16[12,256,256]{2,1,0:T(8,128)(2,1)}, bf16[12,256,256]{2,1,0:T(8,128)(2,1)S(1)}, u32[]{:S(2)}) copy-start(bf16[12,256,256]{2,1,0:T(8,128)(2,1)S(1)} %collective-permute-done.4.refs_7_.refs_4_) | copy-start | bytes 4718596
  59.9 9.0 %collective-permute-start.7 = (bf16[8,256,256]{2,1,0:T(8,128)(2,1)}, bf16[8,256,256]{2,1,0:T(8,128)(2,1)S(1)}, u32[]{:S(2)}, u32[]{:S(2)}) collective-permute-start(bf16[8,256,256]{2,1,0:T(8,128)(2,1)} %bitcast.9), channel_id=1, source_target_pairs={{0,1},{1,0},{2,3},{3,2},{4,5},{5,4},{6,7},{7,6},{8,9},{9,8},{10,11... | collective-permute-start | bytes 3145736 | tf_op jit(solution)/shard_map/ppermute | solution.py:129

commit v3 on v2

v3 whole, which is shorter than its diff:
```python
import functools

import jax
import jax.numpy as jnp
from jax import lax
from jax.experimental import pallas as pl
from jax.experimental.pallas import tpu as pltpu
from jax.sharding import PartitionSpec as P


def source_of(delta, parity, own_job, phase):
    d = jnp.clip(delta, -1, 1)
    outer = 2 * parity - 1
    if own_job:
        if phase == 0:
            return jnp.where(d == 0, 0, jnp.where(d == -outer, 1, 2))
        return jnp.where(d == outer, 0, 2)
    if phase == 0:
        return jnp.where(d == 0, 1, jnp.where(d == outer, 0, 2))
    return jnp.where(d == -outer, 0, 2)


def pairs_kernel(phase, jobs, n_src, half, *refs):
    njobs = len(jobs)
    ints = refs[:2 * njobs]
    srcs = refs[2 * njobs:2 * njobs + n_src]
    ops = refs[2 * njobs + n_src:4 * njobs + n_src]
    rest = refs[4 * njobs + n_src:]
    starts = rest[:njobs] if phase > 0 else (None,) * njobs
    rest = rest[njobs:] if phase > 0 else rest
    outs, (acc_ref, mixed_ref) = rest[:njobs], rest[njobs:]
    width = srcs[0].shape[1]
    parity = lax.axis_index("sector") % 2
    for j, own_job in enumerate(jobs):
        deltas_ref, count_ref = ints[2 * j], ints[2 * j + 1]
        left_ref, right_ref = ops[2 * j], ops[2 * j + 1]
        start_ref, out_ref = starts[j], outs[j]
        first = 0 if (phase > 0 or own_job) else half
        if start_ref is None:
            acc_ref[...] = jnp.zeros_like(acc_ref)
        else:
            acc_ref[...] = start_ref[...]

        def step(k, carry, deltas_ref=deltas_ref, left_ref=left_ref, right_ref=right_ref, own_job=own_job, first=first):
            which = source_of(deltas_ref[k], parity, own_job, phase)

            @pl.when(which < n_src)
            def _():
                left = left_ref[k]

                def run(src_ref):
                    for r in range(half):
                        mixed_ref[pl.ds(r * width, width), :] = jnp.dot(
                            left, src_ref[first + r], preferred_element_type=jnp.float32
                        ).astype(jnp.bfloat16)

                for m, ref in enumerate(srcs):
                    pl.when(which == m)(functools.partial(run, ref))
                acc_ref[...] += lax.dot_general(
                    mixed_ref[...], right_ref[k], (((1,), (1,)), ((), ())), preferred_element_type=jnp.float32
                )

            return carry

        lax.fori_loop(0, jnp.minimum(count_ref[0], left_ref.shape[0]), step, 0)
        if phase > 0 and own_job:
            out_ref[pl.ds(0, half * width), :] = acc_ref[...].astype(out_ref.dtype)
        else:
            out_ref[...] = acc_ref[...].astype(out_ref.dtype)


def apply_pairs(phase, sources, jobs, half, starts=()):
    width = sources[0].shape[1]
    size = half * width
    slots = jobs[0][1][0].shape[0]
    vmem = pl.BlockSpec(memory_space=pltpu.VMEM)
    smem = pl.BlockSpec(memory_space=pltpu.SMEM)
    flops = 2 * slots * size * width * width * len(jobs) // 3
    moved = 2 * (len(sources) * size * width + 2 * len(jobs) * slots * width * width) + 8 * len(jobs) * size * width
    outs = []
    for is_own, _ in jobs:
        if phase == 0:
            outs.append(jax.ShapeDtypeStruct((size, width), jnp.float32))
        else:
            outs.append(jax.ShapeDtypeStruct(((2 if is_own else 1) * size, width), jnp.bfloat16))
    ints = [x for _, (l, r, d, c) in jobs for x in (d, c)]
    ops = [x for _, (l, r, d, c) in jobs for x in (l, r)]
    return pl.pallas_call(
        functools.partial(pairs_kernel, phase, tuple(o for o, _ in jobs), len(sources), half),
        out_shape=tuple(outs),
        in_specs=[smem] * len(ints) + [vmem] * (len(sources) + len(ops) + len(starts)),
        out_specs=tuple(vmem for _ in outs),
        scratch_shapes=[
            pltpu.VMEM((size, width), jnp.float32),
            pltpu.VMEM((size, width), jnp.bfloat16),
        ],
        cost_estimate=pl.CostEstimate(flops=flops, bytes_accessed=moved, transcendentals=0),
    )(*ints, *sources, *ops, *starts)


def on_device(wave, left_ops, right_ops, deltas, counts):
    n = lax.axis_size("sector")
    own = wave[0]
    half = own.shape[0] // 2

    odd, even = range(1, n, 2), range(0, n, 2)
    near = [(j, j + 1) for j in odd if j + 1 < n] + [(j, j - 1) for j in even if j >= 2]
    far = [(j, j + 2) for j in odd if j + 2 < n] + [(j, j - 2) for j in even if j >= 2]
    partner = [(j, j ^ 1) for j in range(n)]

    from_near = lax.ppermute(own[:half], "sector", near)
    from_far = lax.ppermute(own[half:], "sector", far)
    from_partner = lax.ppermute(own, "sector", partner)

    left_p = lax.ppermute(left_ops, "sector", partner)
    right_p = lax.ppermute(right_ops, "sector", partner)
    deltas_p = lax.ppermute(deltas, "sector", partner)
    counts_p = lax.ppermute(counts, "sector", partner)
    own_job = (left_ops, right_ops, deltas, counts)
    partner_job = (left_p, right_p, deltas_p, counts_p)

    partner_sum, own_sum = apply_pairs(0, (own, from_partner), ((False, partner_job), (True, own_job)), half)
    own_sum, partner_sum, from_near = lax.optimization_barrier((own_sum, partner_sum, from_near))
    (out,) = apply_pairs(1, (from_near,), ((True, own_job),), half, (own_sum,))
    out, partner_sum, from_far = lax.optimization_barrier((out, partner_sum, from_far))
    (partner_half,) = apply_pairs(2, (from_far,), ((False, partner_job),), half, (partner_sum,))

    returned = lax.ppermute(partner_half.reshape((half,) + own.shape[1:]), "sector", partner)
    out = lax.dynamic_update_slice_in_dim(out.reshape(own.shape), returned, half, 0)
    return out[None]


def solution(mesh):
    return jax.shard_map(
        on_device,
        mesh=mesh,
        in_specs=(
            P(("group", "sector"), None, None, None),
            P(("group", "sector"), None, None),
            P(("group", "sector"), None, None),
            P(("group", "sector")),
            P(("group", "sector")),
        ),
        out_specs=P(("group", "sector"), None, None, None),
        check_vma=False,
    )
```

time: 69.3 us -> 68.5 us (0.988)
  the two profiles are of different devices: /device:TPU:19 before, /device:TPU:15 now
where the time goes in v3:
time: 68.5 us; the launch traced here: 67.8 us
  Pallas kernels  30.2 us (44%)
  waiting for transfers between devices  18.4 us (27%)
  starting transfers between devices  12.7 us (19%)
  local copies, waits for them, and re-layouts  5.76 us (8%)
  between operations  0.73 us (1%)
    pallas_call x3, Pallas kernels, apply_pairs(): pl.pallas_call(functools.partial(pairs_kernel, phase, tuple((o for o, _ i...  30.2 us
    ppermute x1, waiting for transfers between devices, on_device(): from_far = lax.ppermute(own[half:], 'sector', far)  13.4 us
    ppermute x1, starting transfers between devices, on_device(): lax.ppermute(partner_half.reshape((half,) + own.shape[1:]), 'sector', par...  4.92 us
    ppermute x1, starting transfers between devices, on_device(): from_far = lax.ppermute(own[half:], 'sector', far)  3.14 us
    ppermute x1, starting transfers between devices, on_device(): from_near = lax.ppermute(own[:half], 'sector', near)  3.09 us
    slice x1, local copies, waits for them, and re-layouts, on_device(): from_far = lax.ppermute(own[half:], 'sector', far)  3.04 us
    ppermute x1, waiting for transfers between devices, on_device(): lax.ppermute(partner_half.reshape((half,) + own.shape[1:]), 'sector', par...  2.5 us
    ppermute x1, waiting for transfers between devices, on_device(): counts_p = lax.ppermute(counts, 'sector', partner)  1.69 us
  transfers between devices with their start and end apart: 8, of which 4 were waited for; matrix products, arithmetic and copies ran while one was open for 4% of the time, Pallas kernels for 36%

profile of v3, /device:TPU:15, one launch (start us, length us, event | category | flops | bytes accessed | tf_op | source)
XLA Modules:
  0.0 67.8 jit_solution(2668725323158446299)
XLA Ops:
  0.0 0.7 collective-permute-start.2
  0.7 0.1 collective-permute-start.3
  0.7 0.4 collective-permute-start.4
  1.2 3.0 %slice_bitcast_fusion = (bf16[8,256,256]{2,1,0:T(8,128)(2,1)}, bf16[8,256,256]{2,1,0:T(8,128)(2,1)}) fusion(bf16[1,16,256,256]{3,2,1,0:T(8,128)(2,1)} %param.5), kind=kLoop, calls=%fused_computation.1 | loop fusion | bytes 4194304 | tf_op jit(solution)/shard_map/slice | solution.py:112
  4.2 3.1 %collective-permute-start.5 = (bf16[8,256,256]{2,1,0:T(8,128)(2,1)}, bf16[8,256,256]{2,1,0:T(8,128)(2,1)}, u32[]{:S(2)}, u32[]{:S(2)}) collective-permute-start(bf16[8,256,256]{2,1,0:T(8,128)(2,1)} %get-tuple-element.22), channel_id=1, source_target_pairs={{1,2},{3,4},{5,6},{7,8},{9,10},{11,12},{13,14},{2,1},{4,3},{6,5},{... | collective-permute-start | bytes 3145736 | tf_op jit(solution)/shard_map/ppermute | solution.py:111
  7.3 0.1 collective-permute-start.1
  7.4 1.7 %collective-permute-done.1.refs_1_ = s32[1]{0:T(128)} collective-permute-done((s32[1]{0:T(128)}, s32[1]{0:T(128)}, u32[]{:S(2)}, u32[]{:S(2)}) %collective-permute-start.1) | collective-permute-done | bytes 36 | tf_op jit(solution)/shard_map/ppermute | solution.py:118
  9.1 0.0 copy-done.2
  9.1 0.3 collective-permute-start
  9.4 0.8 %collective-permute-done.refs_0_ = s32[12]{0:T(128)S(1)} collective-permute-done((s32[12]{0:T(128)S(1)}, s32[12]{0:T(128)S(1)}, u32[]{:S(2)}, u32[]{:S(2)}) %collective-permute-start) | collective-permute-done | bytes 80 | tf_op jit(solution)/shard_map/ppermute | solution.py:117
  10.2 3.1 %collective-permute-start.6 = (bf16[8,256,256]{2,1,0:T(8,128)(2,1)}, bf16[8,256,256]{2,1,0:T(8,128)(2,1)}, u32[]{:S(2)}, u32[]{:S(2)}) collective-permute-start(bf16[8,256,256]{2,1,0:T(8,128)(2,1)} %get-tuple-element.21), channel_id=1, source_target_pairs={{1,3},{3,5},{5,7},{7,9},{9,11},{11,13},{13,15},{2,0},{4,2},{6,4},{... | collective-permute-start | bytes 3145736 | tf_op jit(solution)/shard_map/ppermute | solution.py:112
  14.0 0.0 collective-permute-done.3.refs_6_.refs_3_
  14.0 0.0 collective-permute-done.4.refs_7_.refs_4_
  14.1 0.0 collective-permute-done.2.refs_5_
  14.1 1.1 %copy-done = bf16[12,256,256]{2,1,0:T(8,128)(2,1)} copy-done((bf16[12,256,256]{2,1,0:T(8,128)(2,1)}, bf16[12,256,256]{2,1,0:T(8,128)(2,1)S(1)}, u32[]{:S(2)}) %copy-start) | copy-done | bytes 1572888
  15.2 0.6 copy-done.1
  15.8 13.6 %shard_map.55 = (f32[2048,256]{1,0:T(8,128)}, f32[2048,256]{1,0:T(8,128)}) custom-call(s32[12]{0:T(128)} %copy-done.3, s32[1]{0:T(128)} %collective-permute-done.1.refs_1_, s32[12]{0:T(128)} %refs_0_.1, s32[1]{0:T(128)S(6)} %copy.7.refs_3_.refs_1_, bf16[16,256,256]{2,1,0:T(8,128)(2,1)} %bitcast.10, bf16[16,256,256]{2,1,0:T(8,128)(2,1)} %collective-permute-done.2.refs_5_, ...), custom_call_target="tpu_custom_call" | custom-call | flops 2147483648 | bytes 16777216 | tf_op jit(solution)/shard_map/pallas_call | solution.py:88
  29.4 0.0 collective-permute-done.5.refs_2_
  29.4 10.9 %shard_map.56 = bf16[4096,256]{1,0:T(8,128)(2,1)} custom-call(s32[12]{0:T(128)} %refs_0_.1, s32[1]{0:T(128)S(6)} %copy.7.refs_3_.refs_1_, bf16[8,256,256]{2,1,0:T(8,128)(2,1)} %collective-permute-done.5.refs_2_, bf16[12,256,256]{2,1,0:T(8,128)(2,1)} %refs_3_.2, bf16[12,256,256]{2,1,0:T(8,128)(2,1)} %refs_4_.1, f32[2048,256]{1,0:T(8,128)} %get-tuple-element.16.refs_5_), custom_call_target="tpu_custom_call" | custom-call | flops 1073741824 | bytes 8388608 | tf_op jit(solution)/shard_map/pallas_call | solution.py:88
  40.3 13.4 %collective-permute-done.6.refs_2_ = bf16[8,256,256]{2,1,0:T(8,128)(2,1)} collective-permute-done((bf16[8,256,256]{2,1,0:T(8,128)(2,1)}, bf16[8,256,256]{2,1,0:T(8,128)(2,1)}, u32[]{:S(2)}, u32[]{:S(2)}) %collective-permute-start.6) | collective-permute-done | bytes 1048608 | tf_op jit(solution)/shard_map/ppermute | solution.py:112
  53.7 5.6 %shard_map.57 = bf16[2048,256]{1,0:T(8,128)(2,1)} custom-call(s32[12]{0:T(128)} %copy-done.3, s32[1]{0:T(128)} %collective-permute-done.1.refs_1_, bf16[8,256,256]{2,1,0:T(8,128)(2,1)} %collective-permute-done.6.refs_2_, bf16[12,256,256]{2,1,0:T(8,128)(2,1)} %copy-done, bf16[12,256,256]{2,1,0:T(8,128)(2,1)} %copy-done.1, f32[2048,256]{1,0:T(8,128)} %get-tuple-element.20.refs_5_), custom_call_target="tpu_custom_call" | custom-call | flops 1073741824 | bytes 8388608 | tf_op jit(solution)/shard_map/pallas_call | solution.py:88
  59.4 4.9 %collective-permute-start.7 = (bf16[8,256,256]{2,1,0:T(8,128)(2,1)}, bf16[8,256,256]{2,1,0:T(8,128)(2,1)S(1)}, u32[]{:S(2)}, u32[]{:S(2)}) collective-permute-start(bf16[8,256,256]{2,1,0:T(8,128)(2,1)} %bitcast.12), channel_id=1, source_target_pairs={{0,1},{1,0},{2,3},{3,2},{4,5},{5,4},{6,7},{7,6},{8,9},{9,8},{10,11... | collective-permute-start | bytes 3145736 | tf_op jit(solution)/shard_map/ppermute | solution.py:128
  64.3 2.5 %collective-permute-done.7 = bf16[8,256,256]{2,1,0:T(8,128)(2,1)S(1)} collective-permute-done((bf16[8,256,256]{2,1,0:T(8,128)(2,1)}, bf16[8,256,256]{2,1,0:T(8,128)(2,1)S(1)}, u32[]{:S(2)}, u32[]{:S(2)}) %collective-permute-start.7) | collective-permute-done | bytes 1048608 | tf_op jit(solution)/shard_map/ppermute | solution.py:128
  66.8 1.0 %bitcast_dynamic-update-slice_fusion = bf16[1,16,256,256]{3,2,1,0:T(8,128)(2,1)} fusion(bf16[1,16,256,256]{3,2,1,0:T(8,128)(2,1)} %bitcast.11, bf16[8,256,256]{2,1,0:T(8,128)(2,1)S(1)} %collective-permute-done.7), kind=kLoop, calls=%fused_computation | loop fusion | bytes 2097152 | tf_op jit(solution)/shard_map/dynamic_update_slice | solution.py:129
  (5 shorter events, 0.0 us)
Async XLA Ops:
  0.0 9.1 %copy-start.2 = (s32[12]{0:T(128)S(1)}, s32[12]{0:T(128)}, u32[]{:S(2)}) copy-start(s32[12]{0:T(128)} %refs_0_.1) | copy-start | bytes 148
  0.0 14.1 %collective-permute-start.2 = (bf16[16,256,256]{2,1,0:T(8,128)(2,1)}, bf16[16,256,256]{2,1,0:T(8,128)(2,1)}, u32[]{:S(2)}, u32[]{:S(2)}) collective-permute-start(bf16[16,256,256]{2,1,0:T(8,128)(2,1)} %bitcast.9), channel_id=1, source_target_pairs={{0,1},{1,0},{2,3},{3,2},{4,5},{5,4},{6,7},{7,6},{8,9},{9,8},{10,11... | collective-permute-start | bytes 6291464 | tf_op jit(solution)/shard_map/ppermute | solution.py:113
  0.7 13.4 %collective-permute-start.3 = (bf16[12,256,256]{2,1,0:T(8,128)(2,1)}, bf16[12,256,256]{2,1,0:T(8,128)(2,1)S(1)}, u32[]{:S(2)}, u32[]{:S(2)}) collective-permute-start(bf16[12,256,256]{2,1,0:T(8,128)(2,1)} %refs_3_.2), channel_id=1, source_target_pairs={{0,1},{1,0},{2,3},{3,2},{4,5},{5,4},{6,7},{7,6},{8,9},{9,8},{10,11... | collective-permute-start | bytes 4718600 | tf_op jit(solution)/shard_map/ppermute | solution.py:115
  0.7 13.3 %collective-permute-start.4 = (bf16[12,256,256]{2,1,0:T(8,128)(2,1)}, bf16[12,256,256]{2,1,0:T(8,128)(2,1)S(1)}, u32[]{:S(2)}, u32[]{:S(2)}) collective-permute-start(bf16[12,256,256]{2,1,0:T(8,128)(2,1)} %refs_4_.1), channel_id=1, source_target_pairs={{0,1},{1,0},{2,3},{3,2},{4,5},{5,4},{6,7},{7,6},{8,9},{9,8},{10,11... | collective-permute-start | bytes 4718600 | tf_op jit(solution)/shard_map/ppermute | solution.py:116
  4.2 25.1 %collective-permute-start.5 = (bf16[8,256,256]{2,1,0:T(8,128)(2,1)}, bf16[8,256,256]{2,1,0:T(8,128)(2,1)}, u32[]{:S(2)}, u32[]{:S(2)}) collective-permute-start(bf16[8,256,256]{2,1,0:T(8,128)(2,1)} %get-tuple-element.22), channel_id=1, source_target_pairs={{1,2},{3,4},{5,6},{7,8},{9,10},{11,12},{13,14},{2,1},{4,3},{6,5},{... | collective-permute-start | bytes 3145736 | tf_op jit(solution)/shard_map/ppermute | solution.py:111
  7.3 1.8 %collective-permute-start.1 = (s32[1]{0:T(128)}, s32[1]{0:T(128)}, u32[]{:S(2)}, u32[]{:S(2)}) collective-permute-start(s32[1]{0:T(128)} %param.9), channel_id=1, source_target_pairs={{0,1},{1,0},{2,3},{3,2},{4,5},{5,4},{6,7},{7,6},{8,9},{9,8},{10,11... | collective-permute-start | bytes 20 | tf_op jit(solution)/shard_map/ppermute | solution.py:118
  9.1 1.1 %collective-permute-start = (s32[12]{0:T(128)S(1)}, s32[12]{0:T(128)S(1)}, u32[]{:S(2)}, u32[]{:S(2)}) collective-permute-start(s32[12]{0:T(128)S(1)} %copy-done.2), channel_id=1, source_target_pairs={{0,1},{1,0},{2,3},{3,2},{4,5},{5,4},{6,7},{7,6},{8,9},{9,8},{10,11... | collective-permute-start | bytes 152 | tf_op jit(solution)/shard_map/ppermute | solution.py:117
  10.2 3.8 %copy-start.3 = (s32[12]{0:T(128)}, s32[12]{0:T(128)S(1)}, u32[]{:S(2)}) copy-start(s32[12]{0:T(128)S(1)} %collective-permute-done.refs_0_) | copy-start | bytes 148
  10.2 43.5 %collective-permute-start.6 = (bf16[8,256,256]{2,1,0:T(8,128)(2,1)}, bf16[8,256,256]{2,1,0:T(8,128)(2,1)}, u32[]{:S(2)}, u32[]{:S(2)}) collective-permute-start(bf16[8,256,256]{2,1,0:T(8,128)(2,1)} %get-tuple-element.21), channel_id=1, source_target_pairs={{1,3},{3,5},{5,7},{7,9},{9,11},{11,13},{13,15},{2,0},{4,2},{6,4},{... | collective-permute-start | bytes 3145736 | tf_op jit(solution)/shard_map/ppermute | solution.py:112
  14.0 1.1 %copy-start = (bf16[12,256,256]{2,1,0:T(8,128)(2,1)}, bf16[12,256,256]{2,1,0:T(8,128)(2,1)S(1)}, u32[]{:S(2)}) copy-start(bf16[12,256,256]{2,1,0:T(8,128)(2,1)S(1)} %collective-permute-done.3.refs_6_.refs_3_) | copy-start | bytes 4718596
  14.1 1.7 %copy-start.1 = (bf16[12,256,256]{2,1,0:T(8,128)(2,1)}, bf16[12,256,256]{2,1,0:T(8,128)(2,1)S(1)}, u32[]{:S(2)}) copy-start(bf16[12,256,256]{2,1,0:T(8,128)(2,1)S(1)} %collective-permute-done.4.refs_7_.refs_4_) | copy-start | bytes 4718596
  59.4 7.4 %collective-permute-start.7 = (bf16[8,256,256]{2,1,0:T(8,128)(2,1)}, bf16[8,256,256]{2,1,0:T(8,128)(2,1)S(1)}, u32[]{:S(2)}, u32[]{:S(2)}) collective-permute-start(bf16[8,256,256]{2,1,0:T(8,128)(2,1)} %bitcast.12), channel_id=1, source_target_pairs={{0,1},{1,0},{2,3},{3,2},{4,5},{5,4},{6,7},{7,6},{8,9},{9,8},{10,11... | collective-permute-start | bytes 3145736 | tf_op jit(solution)/shard_map/ppermute | solution.py:128

commit v4 on v3

--- a/solution.py
+++ b/solution.py
@@ -112,10 +112,11 @@
     from_far = lax.ppermute(own[half:], "sector", far)
     from_partner = lax.ppermute(own, "sector", partner)
 
-    left_p = lax.ppermute(left_ops, "sector", partner)
-    right_p = lax.ppermute(right_ops, "sector", partner)
-    deltas_p = lax.ppermute(deltas, "sector", partner)
-    counts_p = lax.ppermute(counts, "sector", partner)
+    slots = left_ops.shape[0]
+    ops_p = lax.ppermute(jnp.concatenate([left_ops, right_ops], 0), "sector", partner)
+    left_p, right_p = ops_p[:slots], ops_p[slots:]
+    ints_p = lax.ppermute(jnp.concatenate([deltas, counts]), "sector", partner)
+    deltas_p, counts_p = ints_p[:slots], ints_p[slots:]
     own_job = (left_ops, right_ops, deltas, counts)
     partner_job = (left_p, right_p, deltas_p, counts_p)
 

time: 68.5 us -> 69.8 us (1.019)
  the two profiles are of different devices: /device:TPU:15 before, /device:TPU:25 now
where the time goes in v4:
time: 69.8 us; the launch traced here: 70.3 us
  Pallas kernels  29.3 us (42%)
  waiting for transfers between devices  18.1 us (26%)
  starting transfers between devices  12.4 us (18%)
  local copies, waits for them, and re-layouts  7.4 us (11%)
  other arithmetic  2.38 us (3%)
    pallas_call x3, Pallas kernels, apply_pairs(): pl.pallas_call(functools.partial(pairs_kernel, phase, tuple((o for o, _ i...  29.3 us
    ppermute x1, waiting for transfers between devices, on_device(): from_near = lax.ppermute(own[:half], 'sector', near)  14.8 us
    ppermute x1, starting transfers between devices, on_device(): lax.ppermute(partner_half.reshape((half,) + own.shape[1:]), 'sector', par...  5.69 us
    ppermute x1, starting transfers between devices, on_device(): from_near = lax.ppermute(own[:half], 'sector', near)  3.37 us
    ppermute x1, waiting for transfers between devices, on_device(): lax.ppermute(partner_half.reshape((half,) + own.shape[1:]), 'sector', par...  2.5 us
    concatenate x1, other arithmetic, on_device(): jnp.concatenate([left_ops, right_ops], 0)  2.3 us
    unnamed x10, local copies, waits for them, and re-layouts  2.29 us
    slice x1, local copies, waits for them, and re-layouts, on_device(): left_p, right_p = (ops_p[:slots], ops_p[slots:])  1.98 us
  transfers between devices with their start and end apart: 6, of which 3 were waited for; matrix products, arithmetic and copies ran while one was open for 6% of the time, Pallas kernels for 34%

profile of v4, /device:TPU:25, one launch (start us, length us, event | category | flops | bytes accessed | tf_op | source)
XLA Modules:
  0.0 70.3 jit_solution(5119174309783900671)
XLA Ops:
  0.0 2.3 %pad_maximum_fusion = bf16[24,256,256]{2,1,0:T(8,128)(2,1)S(1)} fusion(bf16[12,256,256]{2,1,0:T(8,128)(2,1)} %refs_4_.1, bf16[12,256,256]{2,1,0:T(8,128)(2,1)} %refs_3_.2), kind=kLoop, calls=%fused_computation | loop fusion | flops 1572864 | bytes 6291456 | tf_op jit(solution)/shard_map/concatenate | solution.py:116
  2.3 0.7 %collective-permute-start.2 = (bf16[24,256,256]{2,1,0:T(8,128)(2,1)S(1)}, bf16[24,256,256]{2,1,0:T(8,128)(2,1)S(1)}, u32[]{:S(2)}, u32[]{:S(2)}) collective-permute-start(bf16[24,256,256]{2,1,0:T(8,128)(2,1)S(1)} %pad_maximum_fusion), channel_id=1, source_target_pairs={{0,1},{1,0},{2,3},{3,2},{4,5},{5,4},{6,7},{7,6},{8,9},{9,8},{10,11... | collective-permute-start | bytes 9437192 | tf_op jit(solution)/shard_map/ppermute | solution.py:116
  3.0 0.0 copy-done
  3.1 0.2 collective-permute-start.1
  3.2 1.5 %slice_bitcast_fusion = (bf16[8,256,256]{2,1,0:T(8,128)(2,1)}, bf16[8,256,256]{2,1,0:T(8,128)(2,1)}) fusion(bf16[1,16,256,256]{3,2,1,0:T(8,128)(2,1)S(1)} %copy-done), kind=kLoop, calls=%fused_computation.2 | loop fusion | bytes 4194304 | tf_op jit(solution)/shard_map/slice | solution.py:112
  4.7 3.4 %collective-permute-start.3 = (bf16[8,256,256]{2,1,0:T(8,128)(2,1)}, bf16[8,256,256]{2,1,0:T(8,128)(2,1)S(1)}, u32[]{:S(2)}, u32[]{:S(2)}) collective-permute-start(bf16[8,256,256]{2,1,0:T(8,128)(2,1)} %get-tuple-element.24), channel_id=1, source_target_pairs={{1,2},{3,4},{5,6},{7,8},{9,10},{11,12},{13,14},{2,1},{4,3},{6,5},{... | collective-permute-start | bytes 3145736 | tf_op jit(solution)/shard_map/ppermute | solution.py:111
  8.1 1.9 %collective-permute-start.4 = (bf16[8,256,256]{2,1,0:T(8,128)(2,1)}, bf16[8,256,256]{2,1,0:T(8,128)(2,1)}, u32[]{:S(2)}, u32[]{:S(2)}) collective-permute-start(bf16[8,256,256]{2,1,0:T(8,128)(2,1)} %get-tuple-element.23), channel_id=1, source_target_pairs={{1,3},{3,5},{5,7},{7,9},{9,11},{11,13},{13,15},{2,0},{4,2},{6,4},{... | collective-permute-start | bytes 3145736 | tf_op jit(solution)/shard_map/ppermute | solution.py:112
  10.7 0.1 pad_add_fusion
  10.8 0.5 collective-permute-start
  11.3 0.8 %collective-permute-done = s32[13]{0:T(128)S(1)} collective-permute-done((s32[13]{0:T(128)S(1)}, s32[13]{0:T(128)S(1)}, u32[]{:S(2)}, u32[]{:S(2)}) %collective-permute-start) | collective-permute-done | bytes 84 | tf_op jit(solution)/shard_map/ppermute | solution.py:118
  12.1 0.6 slice.25.refs_1_
  12.7 0.0 collective-permute-done.2
  12.7 2.0 %fusion = (bf16[12,256,256]{2,1,0:T(8,128)(2,1)}, bf16[12,256,256]{2,1,0:T(8,128)(2,1)}) fusion(bf16[24,256,256]{2,1,0:T(8,128)(2,1)S(1)} %collective-permute-done.2), kind=kLoop, calls=%fused_computation.5 | loop fusion | bytes 6291456 | tf_op jit(solution)/shard_map/slice | solution.py:117
  14.7 0.0 collective-permute-done.1.refs_5_
  14.7 1.3 %copy-done.1 = bf16[16,256,256]{2,1,0:T(8,128)(2,1)} copy-done((bf16[16,256,256]{2,1,0:T(8,128)(2,1)}, bf16[16,256,256]{2,1,0:T(8,128)(2,1)S(1)}, u32[]{:S(2)}) %copy-start.1) | copy-done | bytes 2097176
  16.0 12.7 %shard_map.55 = (f32[2048,256]{1,0:T(8,128)}, f32[2048,256]{1,0:T(8,128)}) custom-call(s32[12]{0:T(128)} %bitcast.14, s32[1]{0:T(128)} %slice.25.refs_1_, s32[12]{0:T(128)} %refs_0_.1, s32[1]{0:T(128)S(6)} %copy.7.refs_3_.refs_1_, bf16[16,256,256]{2,1,0:T(8,128)(2,1)} %bitcast.10, bf16[16,256,256]{2,1,0:T(8,128)(2,1)} %copy-done.1, ...), custom_call_target="tpu_custom_call" | custom-call | flops 2147483648 | bytes 16777216 | tf_op jit(solution)/shard_map/pallas_call | solution.py:88
  28.7 14.8 %collective-permute-done.3.refs_2_ = bf16[8,256,256]{2,1,0:T(8,128)(2,1)S(1)} collective-permute-done((bf16[8,256,256]{2,1,0:T(8,128)(2,1)}, bf16[8,256,256]{2,1,0:T(8,128)(2,1)S(1)}, u32[]{:S(2)}, u32[]{:S(2)}) %collective-permute-start.3) | collective-permute-done | bytes 1048608 | tf_op jit(solution)/shard_map/ppermute | solution.py:111
  43.5 1.0 %copy-done.2 = bf16[8,256,256]{2,1,0:T(8,128)(2,1)} copy-done((bf16[8,256,256]{2,1,0:T(8,128)(2,1)}, bf16[8,256,256]{2,1,0:T(8,128)(2,1)S(1)}, u32[]{:S(2)}) %copy-start.2) | copy-done | bytes 1048600
  44.5 11.0 %shard_map.56 = bf16[4096,256]{1,0:T(8,128)(2,1)} custom-call(s32[12]{0:T(128)} %refs_0_.1, s32[1]{0:T(128)S(6)} %copy.7.refs_3_.refs_1_, bf16[8,256,256]{2,1,0:T(8,128)(2,1)} %copy-done.2, bf16[12,256,256]{2,1,0:T(8,128)(2,1)} %refs_3_.2, bf16[12,256,256]{2,1,0:T(8,128)(2,1)} %refs_4_.1, f32[2048,256]{1,0:T(8,128)} %get-tuple-element.16.refs_5_), custom_call_target="tpu_custom_call" | custom-call | flops 1073741824 | bytes 8388608 | tf_op jit(solution)/shard_map/pallas_call | solution.py:88
  55.4 0.0 collective-permute-done.4.refs_2_
  55.4 5.6 %shard_map.57 = bf16[2048,256]{1,0:T(8,128)(2,1)} custom-call(s32[12]{0:T(128)} %bitcast.15, s32[1]{0:T(128)} %slice.25.refs_1_, bf16[8,256,256]{2,1,0:T(8,128)(2,1)} %collective-permute-done.4.refs_2_, bf16[12,256,256]{2,1,0:T(8,128)(2,1)} %get-tuple-element.22.refs_6_.refs_3_, bf16[12,256,256]{2,1,0:T(8,128)(2,1)} %get-tuple-element.21.refs_7_.refs_4_, ...), custom_call_target="tpu_custom_call" | custom-call | flops 1073741824 | bytes 8388608 | tf_op jit(solution)/shard_map/pallas_call | solution.py:88
  61.1 5.7 %collective-permute-start.5 = (bf16[8,256,256]{2,1,0:T(8,128)(2,1)}, bf16[8,256,256]{2,1,0:T(8,128)(2,1)S(1)}, u32[]{:S(2)}, u32[]{:S(2)}) collective-permute-start(bf16[8,256,256]{2,1,0:T(8,128)(2,1)} %bitcast.13), channel_id=1, source_target_pairs={{0,1},{1,0},{2,3},{3,2},{4,5},{5,4},{6,7},{7,6},{8,9},{9,8},{10,11... | collective-permute-start | bytes 3145736 | tf_op jit(solution)/shard_map/ppermute | solution.py:129
  66.8 2.5 %collective-permute-done.5 = bf16[8,256,256]{2,1,0:T(8,128)(2,1)S(1)} collective-permute-done((bf16[8,256,256]{2,1,0:T(8,128)(2,1)}, bf16[8,256,256]{2,1,0:T(8,128)(2,1)S(1)}, u32[]{:S(2)}, u32[]{:S(2)}) %collective-permute-start.5) | collective-permute-done | bytes 1048608 | tf_op jit(solution)/shard_map/ppermute | solution.py:129
  69.2 1.0 %bitcast_dynamic-update-slice_fusion = bf16[1,16,256,256]{3,2,1,0:T(8,128)(2,1)} fusion(bf16[1,16,256,256]{3,2,1,0:T(8,128)(2,1)} %bitcast.12, bf16[8,256,256]{2,1,0:T(8,128)(2,1)S(1)} %collective-permute-done.5), kind=kLoop, calls=%fused_computation.1 | loop fusion | bytes 2097152 | tf_op jit(solution)/shard_map/dynamic_update_slice | solution.py:130
  (7 shorter events, 0.0 us)
Async XLA Ops:
  0.0 3.1 %copy-start = (bf16[1,16,256,256]{3,2,1,0:T(8,128)(2,1)S(1)}, bf16[1,16,256,256]{3,2,1,0:T(8,128)(2,1)}, u32[]{:S(2)}) copy-start(bf16[1,16,256,256]{3,2,1,0:T(8,128)(2,1)} %param.5) | copy-start | bytes 6291460
  2.3 10.4 %collective-permute-start.2 = (bf16[24,256,256]{2,1,0:T(8,128)(2,1)S(1)}, bf16[24,256,256]{2,1,0:T(8,128)(2,1)S(1)}, u32[]{:S(2)}, u32[]{:S(2)}) collective-permute-start(bf16[24,256,256]{2,1,0:T(8,128)(2,1)S(1)} %pad_maximum_fusion), channel_id=1, source_target_pairs={{0,1},{1,0},{2,3},{3,2},{4,5},{5,4},{6,7},{7,6},{8,9},{9,8},{10,11... | collective-permute-start | bytes 9437192 | tf_op jit(solution)/shard_map/ppermute | solution.py:116
  3.1 7.6 %copy-start.3 = (s32[12]{0:T(128)S(1)}, s32[12]{0:T(128)}, u32[]{:S(2)}) copy-start(s32[12]{0:T(128)} %refs_0_.1) | copy-start | bytes 148
  3.1 11.7 %collective-permute-start.1 = (bf16[16,256,256]{2,1,0:T(8,128)(2,1)S(1)}, bf16[16,256,256]{2,1,0:T(8,128)(2,1)S(1)}, u32[]{:S(2)}, u32[]{:S(2)}) collective-permute-start(bf16[16,256,256]{2,1,0:T(8,128)(2,1)S(1)} %bitcast.11), channel_id=1, source_target_pairs={{0,1},{1,0},{2,3},{3,2},{4,5},{5,4},{6,7},{7,6},{8,9},{9,8},{10,11... | collective-permute-start | bytes 6291464 | tf_op jit(solution)/shard_map/ppermute | solution.py:113
  4.7 38.8 %collective-permute-start.3 = (bf16[8,256,256]{2,1,0:T(8,128)(2,1)}, bf16[8,256,256]{2,1,0:T(8,128)(2,1)S(1)}, u32[]{:S(2)}, u32[]{:S(2)}) collective-permute-start(bf16[8,256,256]{2,1,0:T(8,128)(2,1)} %get-tuple-element.24), channel_id=1, source_target_pairs={{1,2},{3,4},{5,6},{7,8},{9,10},{11,12},{13,14},{2,1},{4,3},{6,5},{... | collective-permute-start | bytes 3145736 | tf_op jit(solution)/shard_map/ppermute | solution.py:111
  8.1 47.3 %collective-permute-start.4 = (bf16[8,256,256]{2,1,0:T(8,128)(2,1)}, bf16[8,256,256]{2,1,0:T(8,128)(2,1)}, u32[]{:S(2)}, u32[]{:S(2)}) collective-permute-start(bf16[8,256,256]{2,1,0:T(8,128)(2,1)} %get-tuple-element.23), channel_id=1, source_target_pairs={{1,3},{3,5},{5,7},{7,9},{9,11},{11,13},{13,15},{2,0},{4,2},{6,4},{... | collective-permute-start | bytes 3145736 | tf_op jit(solution)/shard_map/ppermute | solution.py:112
  10.8 1.4 %collective-permute-start = (s32[13]{0:T(128)S(1)}, s32[13]{0:T(128)S(1)}, u32[]{:S(2)}, u32[]{:S(2)}) collective-permute-start(s32[13]{0:T(128)S(1)} %pad_add_fusion), channel_id=1, source_target_pairs={{0,1},{1,0},{2,3},{3,2},{4,5},{5,4},{6,7},{7,6},{8,9},{9,8},{10,11... | collective-permute-start | bytes 164 | tf_op jit(solution)/shard_map/ppermute | solution.py:118
  12.1 2.6 %copy-start.4 = (s32[13]{0:T(128)}, s32[13]{0:T(128)S(1)}, u32[]{:S(2)}) copy-start(s32[13]{0:T(128)S(1)} %collective-permute-done) | copy-start | bytes 160
  14.7 1.3 %copy-start.1 = (bf16[16,256,256]{2,1,0:T(8,128)(2,1)}, bf16[16,256,256]{2,1,0:T(8,128)(2,1)S(1)}, u32[]{:S(2)}) copy-start(bf16[16,256,256]{2,1,0:T(8,128)(2,1)S(1)} %collective-permute-done.1.refs_5_) | copy-start | bytes 6291460
  43.5 1.0 %copy-start.2 = (bf16[8,256,256]{2,1,0:T(8,128)(2,1)}, bf16[8,256,256]{2,1,0:T(8,128)(2,1)S(1)}, u32[]{:S(2)}) copy-start(bf16[8,256,256]{2,1,0:T(8,128)(2,1)S(1)} %collective-permute-done.3.refs_2_) | copy-start | bytes 3145732
  61.1 8.2 %collective-permute-start.5 = (bf16[8,256,256]{2,1,0:T(8,128)(2,1)}, bf16[8,256,256]{2,1,0:T(8,128)(2,1)S(1)}, u32[]{:S(2)}, u32[]{:S(2)}) collective-permute-start(bf16[8,256,256]{2,1,0:T(8,128)(2,1)} %bitcast.13), channel_id=1, source_target_pairs={{0,1},{1,0},{2,3},{3,2},{4,5},{5,4},{6,7},{7,6},{8,9},{9,8},{10,11... | collective-permute-start | bytes 3145736 | tf_op jit(solution)/shard_map/ppermute | solution.py:129
